TPU v7x, 256 devices: a whole 4x4x8 slice. The times are simulated.
256 devices in a mesh: dp: 8 (over x_hi, y), seq: 32 (over x_lo, z, core).
Axes of the slice: x: 4 (x_hi: 2, x_lo: 2; x = x_hi * 2 + x_lo), y: 4, z: 8, core: 2. Of those that a mesh axis runs over, the one named last changes fastest.
Arguments:
- tokens: bfloat16 [8, 12288, 2048], P('dp', 'seq'), may hold values from -32 to 32
- w_qkv: bfloat16 [2048, 3072], P(('dp', 'seq')), may hold values from -1 to 1
- w_out: bfloat16 [1024, 2048], P(('dp', 'seq')), may hold values from -0.1875 to 0.1875
Outputs:
- mixed: bfloat16 [8, 12288, 2048], P('dp', 'seq')
All inputs are finite; a program needn't handle non-finite values.
Results may differ from a plain program's by a relative error of at most 0.007.
Values may be sent and summed in bfloat16 or wider, within the bound.
No kernel may reach another device: no remote copies, remote signals or barrier semaphores. Data moves between devices by JAX's collectives and lax.ppermute only.
A program may use at most 64 MiB of HBM per device.

v0:
```python
import math

import jax
import jax.numpy as jnp
from jax import lax
from jax.sharding import Mesh
from jax.sharding import PartitionSpec as P

HEADS = 8
HEAD_DIM = 128
COLS = 96
AXES = ("xh", "y", "xl", "z", "c")
SPLIT = (2, 4, 2, 8, 2)
X = ("xh", "xl")
SEQ = ("xl", "z", "c")


def ring(block, axis, n):
    idx = lax.axis_index(axis)
    buf = jnp.zeros((n,) + block.shape, block.dtype)
    buf = lax.dynamic_update_index_in_dim(buf, block, idx, 0)
    fwd = bwd = block
    for s in range(1, n // 2 + 1):
        fwd = lax.ppermute(fwd, axis, [(i, (i + 1) % n) for i in range(n)])
        buf = lax.dynamic_update_index_in_dim(buf, fwd, (idx + n - s) % n, 0)
        if s < n - s:
            bwd = lax.ppermute(bwd, axis, [(i, (i - 1) % n) for i in range(n)])
            buf = lax.dynamic_update_index_in_dim(buf, bwd, (idx + s) % n, 0)
    return buf


DIMS = {"y": (2,), "z": (4,), X: (1, 3)}
SIZE = {"z": 8, "y": 4, X: 4}
PARTS = (("y", X), (X, "y"))


def rings(buf, axes):
    for axis in axes:
        buf = ring(buf, axis, SIZE[axis])
    return buf


def with_other(own):
    return own, lax.ppermute(own, "c", [(0, 1), (1, 0)])


def flat_rows(pair, cols):
    return tuple(a.reshape(-1, cols) for a in pair)


def order_of(axes):
    return tuple(reversed(axes))


def by_core(left, per_device, order):
    t = left.reshape(left.shape[0], *SPLIT, per_device)
    inner = tuple(d for axis in order for d in DIMS[axis])
    t = jnp.transpose(t, (0, 5) + inner + (6,))
    t = t.reshape(left.shape[0], 2, -1)
    c = lax.axis_index("c")
    own = lax.dynamic_index_in_dim(t, c, 1, keepdims=False)
    other = lax.dynamic_index_in_dim(t, 1 - c, 1, keepdims=False)
    return own, other


def project(left, per_device, gathered, order):
    own_w, other_w = gathered
    own, other = by_core(left, per_device, order)
    return jnp.dot(own, own_w, preferred_element_type=jnp.float32) + jnp.dot(
        other, other_w, preferred_element_type=jnp.float32
    )


def attend(query, keys, values, allowed):
    scores = jnp.einsum(
        "shqd,shkd->shqk", query, keys, preferred_element_type=jnp.float32
    ) / math.sqrt(query.shape[-1])
    scores = jnp.where(allowed, scores, -jnp.inf)
    top = jnp.max(scores, axis=-1, keepdims=True)
    expo = jnp.exp(scores - top)
    weights = (expo / jnp.sum(expo, axis=-1, keepdims=True)).astype(jnp.bfloat16)
    return jnp.einsum(
        "shqk,shkd->shqd", weights, values, preferred_element_type=jnp.float32
    ).astype(jnp.bfloat16)


def column_heads(packed):
    seq_count, grid_rows, local_cols, count, width = packed.shape
    length = grid_rows * local_cols
    flat = packed.reshape(seq_count, length, count, 3, width // 3)
    flat = jnp.transpose(flat, (0, 2, 3, 1, 4))
    places = jnp.arange(length)
    allowed = (places[:, None] % local_cols == places[None, :] % local_cols) & (
        places[:, None] >= places[None, :]
    )
    result = attend(flat[:, :, 0], flat[:, :, 1], flat[:, :, 2], allowed)
    result = jnp.transpose(result, (0, 2, 1, 3)).reshape(
        seq_count, grid_rows, local_cols, count, width // 3
    )
    return lax.all_to_all(result, SEQ, split_axis=1, concat_axis=2, tiled=True)


def on_device(tokens, w_qkv, w_out):
    seq_count, tok_count, width = tokens.shape
    flat = tokens.reshape(seq_count * tok_count, width)
    half = HEADS // 2
    packed = w_out.reshape(w_qkv.shape[0], -1)
    both = jnp.concatenate([w_qkv, packed], axis=1)
    spread = jnp.broadcast_to(both[None], (SIZE["z"],) + both.shape)
    along_z = lax.all_to_all(spread, "z", 0, 0, tiled=True)
    step = both.shape[1] // len(PARTS)
    spare = both.shape[1] - w_qkv.shape[1]
    pieces, tail = [], None
    for p, axes in enumerate(PARTS):
        own, other = with_other(rings(along_z[..., p * step:(p + 1) * step], axes))
        order = order_of(("z",) + axes)
        if p == len(PARTS) - 1:
            width = step - spare
            tail = (own[..., width:], other[..., width:]), order
            own, other = own[..., :width], other[..., :width]
        gathered = flat_rows((own, other), own.shape[-1])
        pieces.append(project(flat, w_qkv.shape[0], gathered, order))
    qkv = jnp.concatenate(pieces, axis=1).astype(jnp.bfloat16)
    (out_own, out_other), out_order = tail
    lead = out_own.shape[:-2]
    out_w = tuple(
        a.reshape(*lead, w_out.shape[0], w_out.shape[1]).reshape(-1, w_out.shape[1])
        for a in (out_own, out_other)
    )
    qkv = qkv.reshape(seq_count, tok_count, HEADS, 3, HEAD_DIM)
    col_packed = qkv[:, :, half:].reshape(seq_count, tok_count // COLS, COLS, half, 3 * HEAD_DIM)
    received = lax.all_to_all(col_packed, SEQ, split_axis=2, concat_axis=1, tiled=True)
    row_part = jnp.transpose(qkv[:, :, :half], (0, 2, 3, 1, 4))
    places = jnp.arange(tok_count)
    row_mask = (places[:, None] // COLS == places[None, :] // COLS) & (
        places[:, None] >= places[None, :]
    )
    row_out = attend(row_part[:, :, 0], row_part[:, :, 1], row_part[:, :, 2], row_mask)
    received, row_out = lax.optimization_barrier((received, row_out))
    col_out = column_heads(received).reshape(seq_count, tok_count, half, HEAD_DIM)
    row_out = jnp.transpose(row_out, (0, 2, 1, 3))
    heads_out = jnp.concatenate([row_out, col_out], axis=2).reshape(
        seq_count * tok_count, HEADS * HEAD_DIM
    )
    mixed = project(heads_out, w_out.shape[0], out_w, out_order)
    return mixed.astype(jnp.bfloat16).reshape(seq_count, tok_count, w_out.shape[1])


def solution(mesh):
    grid = Mesh(mesh.devices.reshape(SPLIT), AXES)
    act = P(("xh", "y"), SEQ, None)
    weight = P(AXES, None)
    return jax.shard_map(
        on_device, mesh=grid, in_specs=(act, weight, weight), out_specs=act, check_vma=False
    )
```

profile of v0, /device:TPU:1, one launch (start us, length us, event | category | flops | bytes accessed | tf_op | source)
XLA Modules:
  0.0 208.3 jit_solution(8629011601568585641)
XLA Ops:
  2.4 9.0 %all-to-all-start = ((bf16[8,8,4096]{2,1,0:T(8,128)(2,1)}), bf16[8,8,4096]{2,1,0:T(8,128)(2,1)S(1)}, u32[]{:S(2)}, u32[]{:S(2)}) async-start(bf16[8,8,4096]{2,1,0:T(8,128)(2,1)} %broadcast_in_dim.80), calls=%async_computation | async-start | bytes 1048576 | tf_op jit(solution)/shard_map/all_to_all | solution.py:110
  11.4 18.0 %all-to-all-done = bf16[8,8,4096]{2,1,0:T(8,128)(2,1)S(1)} async-done(((bf16[8,8,4096]{2,1,0:T(8,128)(2,1)}), bf16[8,8,4096]{2,1,0:T(8,128)(2,1)S(1)}, u32[]{:S(2)}, u32[]{:S(2)}) %all-to-all-start) | async-done | bytes 524320 | tf_op jit(solution)/shard_map/all_to_all | solution.py:110
  29.4 1.4 collective-permute-start
  30.7 1.5 collective-permute-start.1
  32.3 1.2 collective-permute-start.7
  33.5 1.5 collective-permute-start.8
  35.2 2.9 %collective-permute-done = bf16[8,8,2048]{2,1,0:T(8,128)(2,1)S(1)} collective-permute-done((bf16[8,8,2048]{2,1,0:T(8,128)(2,1)S(1)}, bf16[8,8,2048]{2,1,0:T(8,128)(2,1)S(1)}, u32[]{:S(2)}, u32[]{:S(2)}) %collective-permute-start) | collective-permute-done | bytes 262176 | tf_op jit(solution)/shard_map/ppermute | solution.py:24
  38.1 2.3 %collective-permute-done.7 = bf16[8,8,2048]{2,1,0:T(8,128)(2,1)S(1)} collective-permute-done((bf16[8,8,2048]{2,1,0:T(8,128)(2,1)S(1)}, bf16[8,8,2048]{2,1,0:T(8,128)(2,1)S(1)}, u32[]{:S(2)}, u32[]{:S(2)}) %collective-permute-start.7) | collective-permute-done | bytes 262176 | tf_op jit(solution)/shard_map/ppermute | solution.py:24
  40.6 5.4 %collective-permute-done.2 = bf16[8,8,2048]{2,1,0:T(8,128)(2,1)S(1)} collective-permute-done((bf16[8,8,2048]{2,1,0:T(8,128)(2,1)S(1)}, bf16[8,8,2048]{2,1,0:T(8,128)(2,1)S(1)}, u32[]{:S(2)}, u32[]{:S(2)}) %collective-permute-start.2) | collective-permute-done | bytes 262176 | tf_op jit(solution)/shard_map/ppermute | solution.py:24
  46.0 1.3 collective-permute-start.3
  47.2 1.5 collective-permute-start.4
  48.8 2.7 %collective-permute-start.11 = (bf16[4,8,8,2048]{3,2,1,0:T(8,128)(2,1)S(1)}, bf16[4,8,8,2048]{3,2,1,0:T(8,128)(2,1)S(1)}, u32[]{:S(2)}, u32[]{:S(2)}) collective-permute-start(bf16[4,8,8,2048]{3,2,1,0:T(8,128)(2,1)S(1)} %bitcast_dynamic-update-slice_fusion.8), channel_id=1, source_target_pairs={{0,96},{32,0},{64,32},{96,64},{1,97},{33,1},{65,33},{97,65},{2,98}... | collective-permute-start | bytes 3145736 | tf_op jit(solution)/shard_map/ppermute | solution.py:27
  51.5 2.4 %broadcast.134.clone.1 = bf16[4,4,8,8,2048]{4,3,2,1,0:T(8,128)(2,1)} broadcast(bf16[]{:T(256)} %constant.156.clone.1), dimensions={} | broadcast | bytes 4194306 | tf_op jit(solution)/shard_map/broadcast.8
  53.9 1.1 bitcast_dynamic-update-slice_fusion.7
  55.1 2.5 %broadcast.134.clone = bf16[4,4,8,8,2048]{4,3,2,1,0:T(8,128)(2,1)} broadcast(bf16[]{:T(256)} %constant.156.clone.1), dimensions={} | broadcast | bytes 4194306 | tf_op jit(solution)/shard_map/broadcast.8
  57.5 1.1 bitcast_dynamic-update-slice_fusion.3
  58.7 11.2 %collective-permute-done.3 = bf16[4,8,8,2048]{3,2,1,0:T(8,128)(2,1)S(1)} collective-permute-done((bf16[4,8,8,2048]{3,2,1,0:T(8,128)(2,1)S(1)}, bf16[4,8,8,2048]{3,2,1,0:T(8,128)(2,1)S(1)}, u32[]{:S(2)}, u32[]{:S(2)}) %collective-permute-start.3) | collective-permute-done | bytes 1048608 | tf_op jit(solution)/shard_map/ppermute | solution.py:24
  70.9 1.1 collective-permute-done.10
  72.0 1.1 bitcast_dynamic-update-slice_fusion.2
  75.2 17.6 %collective-permute-done.5 = bf16[4,8,8,2048]{3,2,1,0:T(8,128)(2,1)S(1)} collective-permute-done((bf16[4,8,8,2048]{3,2,1,0:T(8,128)(2,1)S(1)}, bf16[4,8,8,2048]{3,2,1,0:T(8,128)(2,1)S(1)}, u32[]{:S(2)}, u32[]{:S(2)}) %collective-permute-start.5) | collective-permute-done | bytes 1048608 | tf_op jit(solution)/shard_map/ppermute | solution.py:24
  92.8 1.1 bitcast_dynamic-update-slice_fusion.4
  93.9 3.8 %collective-permute-start.6 = (bf16[4,4,8,8,2048]{4,3,2,1,0:T(8,128)(2,1)}, bf16[4,4,8,8,2048]{4,3,2,1,0:T(8,128)(2,1)}, u32[]{:S(2)}, u32[]{:S(2)}) collective-permute-start(bf16[4,4,8,8,2048]{4,3,2,1,0:T(8,128)(2,1)} %bitcast_dynamic-update-slice_fusion.4), channel_id=1, source_target_pairs={{0,1},{1,0},{2,3},{3,2},{4,5},{5,4},{6,7},{7,6},{8,9},{9,8},{10,11... | collective-permute-start | bytes 12582920 | tf_op jit(solution)/shard_map/ppermute | solution.py:44
  98.7 1.1 collective-permute-start.13
  100.7 1.4 copy.53
  102.5 4.3 %fusion.52 = (bf16[4,4,8,8,1024]{4,3,2,1,0:T(8,128)(2,1)}, bf16[4,4,8,8,1024]{4,3,2,1,0:T(8,128)(2,1)S(1)}) fusion(bf16[4,4,8,8,2048]{4,3,2,1,0:T(8,128)(2,1)} %bitcast_dynamic-update-slice_fusion), kind=kLoop, calls=%fused_computation.94 | loop fusion | bytes 8388608 | tf_op jit(solution)/shard_map/slice | solution.py:119
  106.7 4.1 %fusion.16 = f32[384,2048]{1,0:T(8,128)S(1)} fusion(bf16[1024,2048]{1,0:T(8,128)(2,1)} %bitcast.14, bf16[384,2,1024]{0,2,1:T(8,128)(2,1)S(1)} %bitcast.186, s32[]{:T(128)S(6)} %select_n.147), kind=kOutput, calls=%fused_computation.38 | convolution fusion | flops 1610612736 | bytes 8126468 | tf_op jit(solution)/shard_map/dot_general | solution.py:69
  110.8 4.1 %fusion.53 = (bf16[4,4,8,8,1024]{4,3,2,1,0:T(8,128)(2,1)S(1)}, bf16[4,4,8,8,1024]{4,3,2,1,0:T(8,128)(2,1)}) fusion(bf16[4,4,8,8,2048]{4,3,2,1,0:T(8,128)(2,1)} %collective-permute-done.13), kind=kLoop, calls=%fused_computation.95 | loop fusion | bytes 8388608 | tf_op jit(solution)/shard_map/slice | solution.py:120
  116.0 4.1 %add_convert_fusion.1 = bf16[384,2048]{1,0:T(8,128)(2,1)S(1)} fusion(f32[384,2048]{1,0:T(8,128)S(1)} %fusion.16, bf16[1024,2048]{1,0:T(8,128)(2,1)} %bitcast.12, bf16[384,2,1024]{0,2,1:T(8,128)(2,1)S(1)} %bitcast.187, s32[]{:T(128)S(6)} %select_n.132), kind=kOutput, calls=%fused_computation.3 | convolution fusion | flops 1612185600 | bytes 9699332 | tf_op jit(solution)/shard_map/dot_general | solution.py:69
  121.2 1.6 pad_maximum_fusion
  122.8 3.0 %copy.59 = bf16[384,3072]{0,1:T(8,128)(2,1)S(1)} copy(bf16[384,3072]{1,0:T(8,128)(2,1)} %pad_maximum_fusion) | data formatting | bytes 4718592 | tf_op jit(solution)/shard_map/concatenate | solution.py:123
  125.8 1.3 fusion.54
  127.1 3.3 %reshape.214 = bf16[1,4,96,4,384]{2,1,4,3,0:T(4,128)(2,1)S(1)} reshape(bf16[1,384,4,3,128]{1,4,3,2,0:T(8,128)(2,1)} %get-tuple-element.14) | data formatting | bytes 2359296 | tf_op jit(solution)/shard_map/reshape | solution.py:131
  130.4 2.2 %copy.61 = bf16[1,4,96,4,384]{4,1,3,0,2:T(4,128)(2,1)} copy(bf16[1,4,96,4,384]{2,1,4,3,0:T(4,128)(2,1)S(1)} %reshape.214) | data formatting | bytes 2359296 | tf_op jit(solution)/shard_map/reshape | solution.py:131
  132.7 4.0 %all-to-all-start.1 = ((bf16[1,4,96,4,384]{4,1,3,0,2:T(4,128)(2,1)}), bf16[1,4,96,4,384]{4,1,3,0,2:T(4,128)(2,1)S(1)}, u32[]{:S(2)}, u32[]{:S(2)}) async-start(bf16[1,4,96,4,384]{4,1,3,0,2:T(4,128)(2,1)} %copy.61), calls=%async_computation.1 | async-start | bytes 2359296 | tf_op jit(solution)/shard_map/all_to_all | solution.py:132
  139.0 1.8 fusion.56
  140.8 3.0 %fusion.5 = bf16[1,4,384,128]{3,2,1,0:T(8,128)(2,1)} fusion(f32[4,384]{1,0:T(4,128)S(1)} %fusion.56, bf16[1,4,3,384,128]{4,3,1,2,0:T(8,128)(2,1)S(1)} %bitcast.192, pred[384,384]{0,1:T(8,128)(4,1)} %fusion.24), kind=kOutput, calls=%fused_computation.17 | convolution fusion | flops 305137536 | bytes 1726464 | tf_op jit(solution)/shard_map/shqk,shkd->shqd/dot_general | solution.py:82
  143.8 22.0 %all-to-all-done.1 = bf16[1,4,96,4,384]{4,1,3,0,2:T(4,128)(2,1)S(1)} async-done(((bf16[1,4,96,4,384]{4,1,3,0,2:T(4,128)(2,1)}), bf16[1,4,96,4,384]{4,1,3,0,2:T(4,128)(2,1)S(1)}, u32[]{:S(2)}, u32[]{:S(2)}) %all-to-all-start.1) | async-done | bytes 1179680 | tf_op jit(solution)/shard_map/all_to_all | solution.py:132
  169.5 2.7 %fusion.6 = bf16[1,384,4,128]{3,1,2,0:T(8,128)(2,1)S(1)} fusion(f32[4,384]{1,0:T(4,128)S(1)} %fusion.57, bf16[1,4,3,384,128]{4,3,1,2,0:T(8,128)(2,1)} %bitcast.194, pred[384,384]{0,1:T(8,128)(4,1)S(1)} %copy-done.6), kind=kOutput, calls=%fused_computation.18 | convolution fusion | flops 305137536 | bytes 1726464 | tf_op jit(solution)/shard_map/shqk,shkd->shqd/dot_general | solution.py:82
  173.3 6.2 %all-to-all-start.2 = ((bf16[1,128,3,4,128]{4,3,2,0,1:T(4,128)(2,1)}), bf16[1,128,3,4,128]{4,3,2,0,1:T(4,128)(2,1)S(1)}, u32[]{:S(2)}, u32[]{:S(2)}) async-start(bf16[1,128,3,4,128]{4,3,2,0,1:T(4,128)(2,1)} %bitcast.46), calls=%async_computation.2 | async-start | bytes 786432 | tf_op jit(solution)/shard_map/all_to_all | solution.py:100
  179.5 2.2 %reshape_reshape.15 = bf16[512,2048]{1,0:T(8,128)(2,1)} reshape(bf16[4,4,8,8,1024]{4,3,2,1,0:T(8,128)(2,1)S(1)} %copy-done) | data formatting | bytes 4194304 | tf_op jit(solution)/shard_map/reshape;reshape | solution.py:127
  181.7 2.7 %reshape_reshape.16 = bf16[512,2048]{1,0:T(8,128)(2,1)S(1)} reshape(bf16[4,4,8,8,1024]{4,3,2,1,0:T(8,128)(2,1)} %get-tuple-element.12) | data formatting | bytes 4194304 | tf_op jit(solution)/shard_map/reshape;reshape | solution.py:127
  184.4 9.1 %all-to-all-done.2 = bf16[1,128,3,4,128]{4,3,2,0,1:T(4,128)(2,1)S(1)} async-done(((bf16[1,128,3,4,128]{4,3,2,0,1:T(4,128)(2,1)}), bf16[1,128,3,4,128]{4,3,2,0,1:T(4,128)(2,1)S(1)}, u32[]{:S(2)}, u32[]{:S(2)}) %all-to-all-start.2) | async-done | bytes 393248 | tf_op jit(solution)/shard_map/all_to_all | solution.py:100
  194.1 1.2 copy.73
  195.2 1.7 reshape_reshape.14
  197.7 2.5 %constant_dynamic-slice_fusion.1 = (bf16[384,1,512]{0,1,2:T(2,128)(2,1)S(1)}, bf16[384,1,512]{0,1,2:T(2,128)(2,1)}) fusion(bf16[384,2,512]{0,1,2:T(2,128)(2,1)S(1)} %bitcast.181, s32[]{:T(128)S(6)} %select_n.132, s32[]{:T(128)S(6)} %select_n.147), kind=kLoop, calls=%fused_computation.69 | loop fusion | bytes 1572872 | tf_op jit(solution)/shard_map/jit(dynamic_index_in_dim)/dynamic_slice | solution.py:61
  200.2 2.9 %copy.76 = bf16[384,1,512]{2,0,1:T(8,128)(2,1)} copy(bf16[384,1,512]{0,1,2:T(2,128)(2,1)} %get-tuple-element.16) | data formatting | bytes 786432 | tf_op jit(solution)/shard_map/jit(dynamic_index_in_dim)/dynamic_slice | solution.py:62
  204.1 2.1 %fusion.27 = f32[384,2048]{1,0:T(8,128)S(1)} fusion(bf16[512,2048]{1,0:T(8,128)(2,1)S(1)} %reshape_reshape.16, bf16[384,1,512]{2,0,1:T(8,128)(2,1)} %copy.76), kind=kOutput, calls=%fused_computation.56 | convolution fusion | flops 805306368 | bytes 5636096 | tf_op jit(solution)/shard_map/dot_general | solution.py:69
  206.2 2.1 %fusion.2 = bf16[1,384,2048]{2,1,0:T(8,128)(2,1)} fusion(f32[384,2048]{1,0:T(8,128)S(1)} %fusion.27, bf16[512,2048]{1,0:T(8,128)(2,1)S(1)} %copy-done.1, bf16[384,1,512]{2,0,1:T(8,128)(2,1)S(1)} %copy.75), kind=kOutput, calls=%fused_computation.4 | convolution fusion | flops 806879232 | bytes 7208960 | tf_op jit(solution)/shard_map/dot_general | solution.py:69
  (65 shorter events, 19.6 us)
Async XLA Ops:
  2.4 27.0 %all-to-all-start = ((bf16[8,8,4096]{2,1,0:T(8,128)(2,1)}), bf16[8,8,4096]{2,1,0:T(8,128)(2,1)S(1)}, u32[]{:S(2)}, u32[]{:S(2)}) async-start(bf16[8,8,4096]{2,1,0:T(8,128)(2,1)} %broadcast_in_dim.80), calls=%async_computation | async-start | bytes 1048576 | tf_op jit(solution)/shard_map/all_to_all | solution.py:110
  29.4 8.8 %collective-permute-start = (bf16[8,8,2048]{2,1,0:T(8,128)(2,1)S(1)}, bf16[8,8,2048]{2,1,0:T(8,128)(2,1)S(1)}, u32[]{:S(2)}, u32[]{:S(2)}) collective-permute-start(bf16[8,8,2048]{2,1,0:T(8,128)(2,1)S(1)} %get-tuple-element.17), channel_id=1, source_target_pairs={{0,32},{32,64},{64,96},{96,0},{1,33},{33,65},{65,97},{97,1},{2,34}... | collective-permute-start | bytes 786440 | tf_op jit(solution)/shard_map/ppermute | solution.py:24
  30.7 9.8 %collective-permute-start.1 = (bf16[8,8,2048]{2,1,0:T(8,128)(2,1)S(1)}, bf16[8,8,2048]{2,1,0:T(8,128)(2,1)S(1)}, u32[]{:S(2)}, u32[]{:S(2)}) collective-permute-start(bf16[8,8,2048]{2,1,0:T(8,128)(2,1)S(1)} %get-tuple-element.17), channel_id=1, source_target_pairs={{0,96},{32,0},{64,32},{96,64},{1,97},{33,1},{65,33},{97,65},{2,98}... | collective-permute-start | bytes 786440 | tf_op jit(solution)/shard_map/ppermute | solution.py:27
  32.3 8.2 %collective-permute-start.7 = (bf16[8,8,2048]{2,1,0:T(8,128)(2,1)S(1)}, bf16[8,8,2048]{2,1,0:T(8,128)(2,1)S(1)}, u32[]{:S(2)}, u32[]{:S(2)}) collective-permute-start(bf16[8,8,2048]{2,1,0:T(8,128)(2,1)S(1)} %get-tuple-element.18), channel_id=1, source_target_pairs={{0,16},{16,128},{128,144},{144,0},{1,17},{17,129},{129,145},{145,1... | collective-permute-start | bytes 786440 | tf_op jit(solution)/shard_map/ppermute | solution.py:24
  33.5 7.1 %collective-permute-start.8 = (bf16[8,8,2048]{2,1,0:T(8,128)(2,1)S(1)}, bf16[8,8,2048]{2,1,0:T(8,128)(2,1)S(1)}, u32[]{:S(2)}, u32[]{:S(2)}) collective-permute-start(bf16[8,8,2048]{2,1,0:T(8,128)(2,1)S(1)} %get-tuple-element.18), channel_id=1, source_target_pairs={{0,144},{16,0},{128,16},{144,128},{1,145},{17,1},{129,17},{145,129... | collective-permute-start | bytes 786440 | tf_op jit(solution)/shard_map/ppermute | solution.py:27
  38.1 7.8 %collective-permute-start.2 = (bf16[8,8,2048]{2,1,0:T(8,128)(2,1)S(1)}, bf16[8,8,2048]{2,1,0:T(8,128)(2,1)S(1)}, u32[]{:S(2)}, u32[]{:S(2)}) collective-permute-start(bf16[8,8,2048]{2,1,0:T(8,128)(2,1)S(1)} %collective-permute-done), channel_id=1, source_target_pairs={{0,32},{32,64},{64,96},{96,0},{1,33},{33,65},{65,97},{97,1},{2,34}... | collective-permute-start | bytes 786440 | tf_op jit(solution)/shard_map/ppermute | solution.py:24
  40.4 8.3 %collective-permute-start.9 = (bf16[8,8,2048]{2,1,0:T(8,128)(2,1)S(1)}, bf16[8,8,2048]{2,1,0:T(8,128)(2,1)S(1)}, u32[]{:S(2)}, u32[]{:S(2)}) collective-permute-start(bf16[8,8,2048]{2,1,0:T(8,128)(2,1)S(1)} %collective-permute-done.7), channel_id=1, source_target_pairs={{0,16},{16,128},{128,144},{144,0},{1,17},{17,129},{129,145},{145,1... | collective-permute-start | bytes 786440 | tf_op jit(solution)/shard_map/ppermute | solution.py:24
  46.0 23.9 %collective-permute-start.3 = (bf16[4,8,8,2048]{3,2,1,0:T(8,128)(2,1)S(1)}, bf16[4,8,8,2048]{3,2,1,0:T(8,128)(2,1)S(1)}, u32[]{:S(2)}, u32[]{:S(2)}) collective-permute-start(bf16[4,8,8,2048]{3,2,1,0:T(8,128)(2,1)S(1)} %bitcast_dynamic-update-slice_fusion.12), channel_id=1, source_target_pairs={{0,16},{16,128},{128,144},{144,0},{1,17},{17,129},{129,145},{145,1... | collective-permute-start | bytes 3145736 | tf_op jit(solution)/shard_map/ppermute | solution.py:24
  47.2 25.9 %collective-permute-start.4 = (bf16[4,8,8,2048]{3,2,1,0:T(8,128)(2,1)S(1)}, bf16[4,8,8,2048]{3,2,1,0:T(8,128)(2,1)S(1)}, u32[]{:S(2)}, u32[]{:S(2)}) collective-permute-start(bf16[4,8,8,2048]{3,2,1,0:T(8,128)(2,1)S(1)} %bitcast_dynamic-update-slice_fusion.12), channel_id=1, source_target_pairs={{0,144},{16,0},{128,16},{144,128},{1,145},{17,1},{129,17},{145,129... | collective-permute-start | bytes 3145736 | tf_op jit(solution)/shard_map/ppermute | solution.py:27
  48.7 23.3 %collective-permute-start.10 = (bf16[4,8,8,2048]{3,2,1,0:T(8,128)(2,1)S(1)}, bf16[4,8,8,2048]{3,2,1,0:T(8,128)(2,1)S(1)}, u32[]{:S(2)}, u32[]{:S(2)}) collective-permute-start(bf16[4,8,8,2048]{3,2,1,0:T(8,128)(2,1)S(1)} %bitcast_dynamic-update-slice_fusion.8), channel_id=1, source_target_pairs={{0,32},{32,64},{64,96},{96,0},{1,33},{33,65},{65,97},{97,1},{2,34}... | collective-permute-start | bytes 3145736 | tf_op jit(solution)/shard_map/ppermute | solution.py:24
  48.8 25.3 %collective-permute-start.11 = (bf16[4,8,8,2048]{3,2,1,0:T(8,128)(2,1)S(1)}, bf16[4,8,8,2048]{3,2,1,0:T(8,128)(2,1)S(1)}, u32[]{:S(2)}, u32[]{:S(2)}) collective-permute-start(bf16[4,8,8,2048]{3,2,1,0:T(8,128)(2,1)S(1)} %bitcast_dynamic-update-slice_fusion.8), channel_id=1, source_target_pairs={{0,96},{32,0},{64,32},{96,64},{1,97},{33,1},{65,33},{97,65},{2,98}... | collective-permute-start | bytes 3145736 | tf_op jit(solution)/shard_map/ppermute | solution.py:27
  69.9 22.9 %collective-permute-start.5 = (bf16[4,8,8,2048]{3,2,1,0:T(8,128)(2,1)S(1)}, bf16[4,8,8,2048]{3,2,1,0:T(8,128)(2,1)S(1)}, u32[]{:S(2)}, u32[]{:S(2)}) collective-permute-start(bf16[4,8,8,2048]{3,2,1,0:T(8,128)(2,1)S(1)} %collective-permute-done.3), channel_id=1, source_target_pairs={{0,16},{16,128},{128,144},{144,0},{1,17},{17,129},{129,145},{145,1... | collective-permute-start | bytes 3145736 | tf_op jit(solution)/shard_map/ppermute | solution.py:24
  72.0 25.7 %collective-permute-start.12 = (bf16[4,8,8,2048]{3,2,1,0:T(8,128)(2,1)S(1)}, bf16[4,8,8,2048]{3,2,1,0:T(8,128)(2,1)S(1)}, u32[]{:S(2)}, u32[]{:S(2)}) collective-permute-start(bf16[4,8,8,2048]{3,2,1,0:T(8,128)(2,1)S(1)} %collective-permute-done.10), channel_id=1, source_target_pairs={{0,32},{32,64},{64,96},{96,0},{1,33},{33,65},{65,97},{97,1},{2,34}... | collective-permute-start | bytes 3145736 | tf_op jit(solution)/shard_map/ppermute | solution.py:24
  75.2 24.7 %copy-start.3 = (bf16[1,384,2048]{2,1,0:T(8,128)(2,1)S(1)}, bf16[1,384,2048]{2,1,0:T(8,128)(2,1)}, u32[]{:S(2)}) copy-start(bf16[1,384,2048]{2,1,0:T(8,128)(2,1)} %param.3) | copy-start | bytes 4718596
  93.9 12.9 %collective-permute-start.6 = (bf16[4,4,8,8,2048]{4,3,2,1,0:T(8,128)(2,1)}, bf16[4,4,8,8,2048]{4,3,2,1,0:T(8,128)(2,1)}, u32[]{:S(2)}, u32[]{:S(2)}) collective-permute-start(bf16[4,4,8,8,2048]{4,3,2,1,0:T(8,128)(2,1)} %bitcast_dynamic-update-slice_fusion.4), channel_id=1, source_target_pairs={{0,1},{1,0},{2,3},{3,2},{4,5},{5,4},{6,7},{7,6},{8,9},{9,8},{10,11... | collective-permute-start | bytes 12582920 | tf_op jit(solution)/shard_map/ppermute | solution.py:44
  98.7 12.1 %collective-permute-start.13 = (bf16[4,4,8,8,2048]{4,3,2,1,0:T(8,128)(2,1)}, bf16[4,4,8,8,2048]{4,3,2,1,0:T(8,128)(2,1)}, u32[]{:S(2)}, u32[]{:S(2)}) collective-permute-start(bf16[4,4,8,8,2048]{4,3,2,1,0:T(8,128)(2,1)} %bitcast_dynamic-update-slice_fusion), channel_id=1, source_target_pairs={{0,1},{1,0},{2,3},{3,2},{4,5},{5,4},{6,7},{7,6},{8,9},{9,8},{10,11... | collective-permute-start | bytes 12582920 | tf_op jit(solution)/shard_map/ppermute | solution.py:44
  102.5 4.3 %copy-start.2 = (bf16[384,2,2,2,4,8,8]{0,6,5,4,3,2,1:T(8,128)(2,1)S(1)}, bf16[384,2,2,2,4,8,8]{0,6,5,4,3,2,1:T(8,128)(2,1)}, u32[]{:S(2)}) copy-start(bf16[384,2,2,2,4,8,8]{0,6,5,4,3,2,1:T(8,128)(2,1)} %copy.53) | copy-start | bytes 4718596
  132.7 33.1 %all-to-all-start.1 = ((bf16[1,4,96,4,384]{4,1,3,0,2:T(4,128)(2,1)}), bf16[1,4,96,4,384]{4,1,3,0,2:T(4,128)(2,1)S(1)}, u32[]{:S(2)}, u32[]{:S(2)}) async-start(bf16[1,4,96,4,384]{4,1,3,0,2:T(4,128)(2,1)} %copy.61), calls=%async_computation.1 | async-start | bytes 2359296 | tf_op jit(solution)/shard_map/all_to_all | solution.py:132
  166.7 2.0 copy-start.6
  167.6 1.0 copy-start.4
  169.5 10.0 %copy-start = (bf16[4,4,8,8,1024]{4,3,2,1,0:T(8,128)(2,1)S(1)}, bf16[4,4,8,8,1024]{4,3,2,1,0:T(8,128)(2,1)}, u32[]{:S(2)}) copy-start(bf16[4,4,8,8,1024]{4,3,2,1,0:T(8,128)(2,1)} %get-tuple-element.9) | copy-start | bytes 6291460
  173.3 20.3 %all-to-all-start.2 = ((bf16[1,128,3,4,128]{4,3,2,0,1:T(4,128)(2,1)}), bf16[1,128,3,4,128]{4,3,2,0,1:T(4,128)(2,1)S(1)}, u32[]{:S(2)}, u32[]{:S(2)}) async-start(bf16[1,128,3,4,128]{4,3,2,0,1:T(4,128)(2,1)} %bitcast.46), calls=%async_computation.2 | async-start | bytes 786432 | tf_op jit(solution)/shard_map/all_to_all | solution.py:100
  181.7 12.3 %copy-start.5 = (bf16[1,4,384,128]{3,2,1,0:T(8,128)(2,1)S(1)}, bf16[1,4,384,128]{3,2,1,0:T(8,128)(2,1)}, u32[]{:S(2)}) copy-start(bf16[1,4,384,128]{3,2,1,0:T(8,128)(2,1)} %fusion.5) | copy-start | bytes 1179652
  204.1 2.1 %copy-start.1 = (bf16[512,2048]{1,0:T(8,128)(2,1)S(1)}, bf16[512,2048]{1,0:T(8,128)(2,1)}, u32[]{:S(2)}) copy-start(bf16[512,2048]{1,0:T(8,128)(2,1)} %reshape_reshape.15) | copy-start | bytes 6291460
where the time goes:
time: 209 us; the launch traced here: 208 us
  waiting for transfers between devices  89.6 us (43%)
  local copies, waits for them, and re-layouts  56.2 us (27%)
  starting transfers between devices  35.3 us (17%)
  matrix products  22.8 us (11%)
  other arithmetic  4.07 us (2%)
    ppermute x8, waiting for transfers between devices, ring(): fwd = lax.ppermute(fwd, axis, [(i, (i + 1) % n) for i in range(n)])  40.5 us
    all_to_all x1, waiting for transfers between devices, on_device(): lax.all_to_all(col_packed, SEQ, split_axis=2, concat_axis=1, tiled=True)  22 us
    all_to_all x1, waiting for transfers between devices, on_device(): along_z = lax.all_to_all(spread, 'z', 0, 0, tiled=True)  18 us
    all_to_all x1, waiting for transfers between devices, column_heads(): return lax.all_to_all(result, SEQ, split_axis=1, concat_axis=2, tiled=True)  9.15 us
    all_to_all x1, starting transfers between devices, on_device(): along_z = lax.all_to_all(spread, 'z', 0, 0, tiled=True)  9 us
    dot_general x3, matrix products, project(): jnp.dot(own, own_w, preferred_element_type=jnp.float32)  7.3 us
    dot_general x3, matrix products, project(): jnp.dot(other, other_w, preferred_element_type=jnp.float32)  7.2 us
    ppermute x4, starting transfers between devices, ring(): bwd = lax.ppermute(bwd, axis, [(i, (i - 1) % n) for i in range(n)])  7.12 us
  transfers between devices with their start and end apart: 17, of which 9 were waited for; matrix products, arithmetic and copies ran while one was open for 18% of the time, Pallas kernels for 0%

commit v1 on v0

--- a/solution.py
+++ b/solution.py
@@ -66,9 +66,9 @@
 def project(left, per_device, gathered, order):
     own_w, other_w = gathered
     own, other = by_core(left, per_device, order)
-    return jnp.dot(own, own_w, preferred_element_type=jnp.float32) + jnp.dot(
-        other, other_w, preferred_element_type=jnp.float32
-    )
+    first = jnp.dot(own, own_w, preferred_element_type=jnp.float32)
+    other_w, first = lax.optimization_barrier((other_w, first))
+    return first + jnp.dot(other, other_w, preferred_element_type=jnp.float32)
 
 
 def attend(query, keys, values, allowed):

time: 209 us -> 208 us (level)
    slice x1 -> x2, local copies, waits for them, and re-layouts: 4.14 us -> 8.4 us  [on_device(): own, other = (own[..., :width], other[..., :width])]
    slice x1 -> x0, local copies, waits for them, and re-layouts: 4.26 us -> none  [on_device(): tail = ((own[..., width:], other[..., width:]), order)]
    dynamic_slice x2 -> x1, local copies, waits for them, and re-layouts: 3.5 us -> 0.99 us  [by_core(): own = lax.dynamic_index_in_dim(t, c, 1, keepdims=False)]
    dynamic_slice x1 -> x2, local copies, waits for them, and re-layouts: 2.85 us -> 4.69 us  [by_core(): other = lax.dynamic_index_in_dim(t, 1 - c, 1, keepdims=False)]
  transfers between devices with their start and end apart: 17 -> 17, of which waited for: 9 -> 9; matrix products, arithmetic and copies ran while one was open for 18% -> 19% of each run, Pallas kernels for 0% -> 0%
where the time goes in v1:
time: 208 us; the launch traced here: 207 us
  waiting for transfers between devices  88.4 us (42%)
  local copies, waits for them, and re-layouts  54.7 us (26%)
  starting transfers between devices  34.7 us (17%)
  matrix products  24.1 us (12%)
  other arithmetic  4.78 us (2%)
    ppermute x8, waiting for transfers between devices, ring(): fwd = lax.ppermute(fwd, axis, [(i, (i + 1) % n) for i in range(n)])  40.4 us
    all_to_all x1, waiting for transfers between devices, on_device(): lax.all_to_all(col_packed, SEQ, split_axis=2, concat_axis=1, tiled=True)  22.2 us
    all_to_all x1, waiting for transfers between devices, on_device(): along_z = lax.all_to_all(spread, 'z', 0, 0, tiled=True)  18 us
    all_to_all x1, starting transfers between devices, on_device(): along_z = lax.all_to_all(spread, 'z', 0, 0, tiled=True)  9 us
    dot_general x3, matrix products, project(): return first + jnp.dot(other, other_w, preferred_element_type=jnp.float32)  8.74 us
    slice x2, local copies, waits for them, and re-layouts, on_device(): own, other = (own[..., :width], other[..., :width])  8.4 us
    all_to_all x1, waiting for transfers between devices, column_heads(): return lax.all_to_all(result, SEQ, split_axis=1, concat_axis=2, tiled=True)  7.77 us
    dot_general x3, matrix products, project(): first = jnp.dot(own, own_w, preferred_element_type=jnp.float32)  7.62 us
  transfers between devices with their start and end apart: 17, of which 9 were waited for; matrix products, arithmetic and copies ran while one was open for 19% of the time, Pallas kernels for 0%

profile of v1, /device:TPU:1, one launch (start us, length us, event | category | flops | bytes accessed | tf_op | source)
XLA Modules:
  0.0 206.9 jit_solution(7017152024827057551)
XLA Ops:
  2.4 9.0 %all-to-all-start = ((bf16[8,8,4096]{2,1,0:T(8,128)(2,1)}), bf16[8,8,4096]{2,1,0:T(8,128)(2,1)S(1)}, u32[]{:S(2)}, u32[]{:S(2)}) async-start(bf16[8,8,4096]{2,1,0:T(8,128)(2,1)} %broadcast_in_dim.80), calls=%async_computation | async-start | bytes 1048576 | tf_op jit(solution)/shard_map/all_to_all | solution.py:110
  11.4 18.0 %all-to-all-done = bf16[8,8,4096]{2,1,0:T(8,128)(2,1)S(1)} async-done(((bf16[8,8,4096]{2,1,0:T(8,128)(2,1)}), bf16[8,8,4096]{2,1,0:T(8,128)(2,1)S(1)}, u32[]{:S(2)}, u32[]{:S(2)}) %all-to-all-start) | async-done | bytes 524320 | tf_op jit(solution)/shard_map/all_to_all | solution.py:110
  29.4 1.4 collective-permute-start.7
  30.7 1.5 collective-permute-start.8
  32.3 1.2 collective-permute-start
  33.5 1.5 collective-permute-start.1
  35.2 2.9 %collective-permute-done.7 = bf16[8,8,2048]{2,1,0:T(8,128)(2,1)S(1)} collective-permute-done((bf16[8,8,2048]{2,1,0:T(8,128)(2,1)S(1)}, bf16[8,8,2048]{2,1,0:T(8,128)(2,1)S(1)}, u32[]{:S(2)}, u32[]{:S(2)}) %collective-permute-start.7) | collective-permute-done | bytes 262176 | tf_op jit(solution)/shard_map/ppermute | solution.py:24
  38.1 2.3 %collective-permute-done = bf16[8,8,2048]{2,1,0:T(8,128)(2,1)S(1)} collective-permute-done((bf16[8,8,2048]{2,1,0:T(8,128)(2,1)S(1)}, bf16[8,8,2048]{2,1,0:T(8,128)(2,1)S(1)}, u32[]{:S(2)}, u32[]{:S(2)}) %collective-permute-start) | collective-permute-done | bytes 262176 | tf_op jit(solution)/shard_map/ppermute | solution.py:24
  40.6 5.4 %collective-permute-done.9 = bf16[8,8,2048]{2,1,0:T(8,128)(2,1)S(1)} collective-permute-done((bf16[8,8,2048]{2,1,0:T(8,128)(2,1)S(1)}, bf16[8,8,2048]{2,1,0:T(8,128)(2,1)S(1)}, u32[]{:S(2)}, u32[]{:S(2)}) %collective-permute-start.9) | collective-permute-done | bytes 262176 | tf_op jit(solution)/shard_map/ppermute | solution.py:24
  46.0 1.3 collective-permute-start.10
  47.2 1.5 collective-permute-start.11
  48.8 2.7 %collective-permute-start.4 = (bf16[4,8,8,2048]{3,2,1,0:T(8,128)(2,1)S(1)}, bf16[4,8,8,2048]{3,2,1,0:T(8,128)(2,1)S(1)}, u32[]{:S(2)}, u32[]{:S(2)}) collective-permute-start(bf16[4,8,8,2048]{3,2,1,0:T(8,128)(2,1)S(1)} %bitcast_dynamic-update-slice_fusion.12), channel_id=1, source_target_pairs={{0,96},{32,0},{64,32},{96,64},{1,97},{33,1},{65,33},{97,65},{2,98}... | collective-permute-start | bytes 3145736 | tf_op jit(solution)/shard_map/ppermute | solution.py:27
  51.5 2.5 %broadcast.134.clone.1 = bf16[4,4,8,8,2048]{4,3,2,1,0:T(8,128)(2,1)} broadcast(bf16[]{:T(256)} %constant.153.clone.1), dimensions={} | broadcast | bytes 4194306 | tf_op jit(solution)/shard_map/broadcast.8
  53.9 1.1 bitcast_dynamic-update-slice_fusion.3
  55.1 2.5 %broadcast.134.clone = bf16[4,4,8,8,2048]{4,3,2,1,0:T(8,128)(2,1)} broadcast(bf16[]{:T(256)} %constant.153.clone.1), dimensions={} | broadcast | bytes 4194306 | tf_op jit(solution)/shard_map/broadcast.8
  57.6 1.1 bitcast_dynamic-update-slice_fusion.7
  58.7 11.1 %collective-permute-done.10 = bf16[4,8,8,2048]{3,2,1,0:T(8,128)(2,1)S(1)} collective-permute-done((bf16[4,8,8,2048]{3,2,1,0:T(8,128)(2,1)S(1)}, bf16[4,8,8,2048]{3,2,1,0:T(8,128)(2,1)S(1)}, u32[]{:S(2)}, u32[]{:S(2)}) %collective-permute-start.10) | collective-permute-done | bytes 1048608 | tf_op jit(solution)/shard_map/ppermute | solution.py:24
  70.9 1.1 collective-permute-done.3
  72.0 1.1 bitcast_dynamic-update-slice_fusion.6
  73.1 1.1 bitcast_dynamic-update-slice_fusion.1
  75.2 17.6 %collective-permute-done.12 = bf16[4,8,8,2048]{3,2,1,0:T(8,128)(2,1)S(1)} collective-permute-done((bf16[4,8,8,2048]{3,2,1,0:T(8,128)(2,1)S(1)}, bf16[4,8,8,2048]{3,2,1,0:T(8,128)(2,1)S(1)}, u32[]{:S(2)}, u32[]{:S(2)}) %collective-permute-start.12) | collective-permute-done | bytes 1048608 | tf_op jit(solution)/shard_map/ppermute | solution.py:24
  93.8 3.8 %collective-permute-start.13 = (bf16[4,4,8,8,2048]{4,3,2,1,0:T(8,128)(2,1)}, bf16[4,4,8,8,2048]{4,3,2,1,0:T(8,128)(2,1)}, u32[]{:S(2)}, u32[]{:S(2)}) collective-permute-start(bf16[4,4,8,8,2048]{4,3,2,1,0:T(8,128)(2,1)} %bitcast_dynamic-update-slice_fusion), channel_id=1, source_target_pairs={{0,1},{1,0},{2,3},{3,2},{4,5},{5,4},{6,7},{7,6},{8,9},{9,8},{10,11... | collective-permute-start | bytes 12582920 | tf_op jit(solution)/shard_map/ppermute | solution.py:44
  97.7 1.1 bitcast_dynamic-update-slice_fusion.4
  98.8 1.1 collective-permute-start.6
  101.0 1.4 copy.56
  102.5 4.2 %fusion.55 = (bf16[4,4,8,8,1024]{4,3,2,1,0:T(8,128)(2,1)S(1)}, bf16[4,4,8,8,1024]{4,3,2,1,0:T(8,128)(2,1)}) fusion(bf16[4,4,8,8,2048]{4,3,2,1,0:T(8,128)(2,1)} %bitcast_dynamic-update-slice_fusion.4), kind=kLoop, calls=%fused_computation.97 | loop fusion | bytes 8388608 | tf_op jit(solution)/shard_map/slice | solution.py:120
  107.7 4.0 %fusion.19 = f32[384,2048]{1,0:T(8,128)S(1)} fusion(bf16[1024,2048]{1,0:T(8,128)(2,1)} %bitcast.21, bf16[384,2,1024]{0,2,1:T(8,128)(2,1)S(1)} %bitcast.186, s32[]{:T(128)S(6)} %select_n.146), kind=kOutput, calls=%fused_computation.41 | convolution fusion | flops 1610612736 | bytes 8126468 | tf_op jit(solution)/shard_map/dot_general | solution.py:69
  111.8 4.2 %fusion.56 = (bf16[4,4,8,8,1024]{4,3,2,1,0:T(8,128)(2,1)S(1)}, bf16[4,4,8,8,1024]{4,3,2,1,0:T(8,128)(2,1)}) fusion(bf16[4,4,8,8,2048]{4,3,2,1,0:T(8,128)(2,1)} %collective-permute-done.6), kind=kLoop, calls=%fused_computation.98 | loop fusion | bytes 8388608 | tf_op jit(solution)/shard_map/slice | solution.py:120
  115.9 4.0 %fusion.17 = f32[384,2048]{1,0:T(8,128)S(1)} fusion(bf16[1024,2048]{1,0:T(8,128)(2,1)} %bitcast.16, bf16[384,2,1024]{0,2,1:T(8,128)(2,1)S(1)} %bitcast.187, s32[]{:T(128)S(6)} %select_n.147), kind=kOutput, calls=%fused_computation.39 | convolution fusion | flops 1610612736 | bytes 8126468 | tf_op jit(solution)/shard_map/dot_general | solution.py:71
  121.7 1.6 pad_maximum_fusion
  123.3 3.0 %copy.59 = bf16[384,3072]{0,1:T(8,128)(2,1)S(1)} copy(bf16[384,3072]{1,0:T(8,128)(2,1)} %pad_maximum_fusion) | data formatting | bytes 4718592 | tf_op jit(solution)/shard_map/concatenate | solution.py:123
  126.3 1.3 fusion.57
  127.7 3.3 %reshape.214 = bf16[1,4,96,4,384]{2,1,4,3,0:T(4,128)(2,1)S(1)} reshape(bf16[1,384,4,3,128]{1,4,3,2,0:T(8,128)(2,1)} %get-tuple-element.26) | data formatting | bytes 2359296 | tf_op jit(solution)/shard_map/reshape | solution.py:131
  131.0 2.2 %copy.61 = bf16[1,4,96,4,384]{4,1,3,0,2:T(4,128)(2,1)} copy(bf16[1,4,96,4,384]{2,1,4,3,0:T(4,128)(2,1)S(1)} %reshape.214) | data formatting | bytes 2359296 | tf_op jit(solution)/shard_map/reshape | solution.py:131
  133.2 3.9 %all-to-all-start.1 = ((bf16[1,4,96,4,384]{4,1,3,0,2:T(4,128)(2,1)}), bf16[1,4,96,4,384]{4,1,3,0,2:T(4,128)(2,1)S(1)}, u32[]{:S(2)}, u32[]{:S(2)}) async-start(bf16[1,4,96,4,384]{4,1,3,0,2:T(4,128)(2,1)} %copy.61), calls=%async_computation.1 | async-start | bytes 2359296 | tf_op jit(solution)/shard_map/all_to_all | solution.py:132
  139.5 1.8 fusion.59
  141.3 3.0 %fusion.5 = bf16[1,4,384,128]{3,2,1,0:T(8,128)(2,1)} fusion(f32[4,384]{1,0:T(4,128)S(1)} %fusion.59, bf16[1,4,3,384,128]{4,3,1,2,0:T(8,128)(2,1)S(1)} %bitcast.196, pred[384,384]{0,1:T(8,128)(4,1)} %fusion.26), kind=kOutput, calls=%fused_computation.17 | convolution fusion | flops 305137536 | bytes 1726464 | tf_op jit(solution)/shard_map/shqk,shkd->shqd/dot_general | solution.py:82
  144.3 22.2 %all-to-all-done.1 = bf16[1,4,96,4,384]{4,1,3,0,2:T(4,128)(2,1)S(1)} async-done(((bf16[1,4,96,4,384]{4,1,3,0,2:T(4,128)(2,1)}), bf16[1,4,96,4,384]{4,1,3,0,2:T(4,128)(2,1)S(1)}, u32[]{:S(2)}, u32[]{:S(2)}) %all-to-all-start.1) | async-done | bytes 1179680 | tf_op jit(solution)/shard_map/all_to_all | solution.py:132
  169.2 2.1 fusion.6
  171.3 2.1 %copy.68 = bf16[1,384,4,128]{3,2,1,0:T(4,128)(2,1)} copy(bf16[1,384,4,128]{3,1,2,0:T(8,128)(2,1)} %fusion.6) | data formatting | bytes 786432 | tf_op jit(solution)/shard_map/transpose | solution.py:97
  173.4 5.7 %all-to-all-start.2 = ((bf16[1,128,3,4,128]{4,3,2,0,1:T(4,128)(2,1)}), bf16[1,128,3,4,128]{4,3,2,0,1:T(4,128)(2,1)S(1)}, u32[]{:S(2)}, u32[]{:S(2)}) async-start(bf16[1,128,3,4,128]{4,3,2,0,1:T(4,128)(2,1)} %bitcast.46), calls=%async_computation.2 | async-start | bytes 786432 | tf_op jit(solution)/shard_map/all_to_all | solution.py:100
  179.0 2.2 %reshape_reshape.16 = bf16[512,2048]{1,0:T(8,128)(2,1)} reshape(bf16[4,4,8,8,1024]{4,3,2,1,0:T(8,128)(2,1)S(1)} %copy-done) | data formatting | bytes 4194304 | tf_op jit(solution)/shard_map/reshape;reshape | solution.py:127
  181.2 4.1 %reshape_reshape.13 = bf16[512,2048]{1,0:T(8,128)(2,1)} reshape(bf16[4,4,8,8,1024]{4,3,2,1,0:T(8,128)(2,1)} %get-tuple-element.24) | data formatting | bytes 4194304 | tf_op jit(solution)/shard_map/reshape;reshape | solution.py:127
  185.3 7.8 %all-to-all-done.2 = bf16[1,128,3,4,128]{4,3,2,0,1:T(4,128)(2,1)S(1)} async-done(((bf16[1,128,3,4,128]{4,3,2,0,1:T(4,128)(2,1)}), bf16[1,128,3,4,128]{4,3,2,0,1:T(4,128)(2,1)S(1)}, u32[]{:S(2)}, u32[]{:S(2)}) %all-to-all-start.2) | async-done | bytes 393248 | tf_op jit(solution)/shard_map/all_to_all | solution.py:100
  194.9 2.5 %constant_dynamic-slice_fusion = (bf16[384,1,512]{0,1,2:T(2,128)(2,1)}, bf16[384,1,512]{0,1,2:T(2,128)(2,1)S(1)}) fusion(bf16[384,2,512]{0,1,2:T(2,128)(2,1)S(1)} %bitcast.185, s32[]{:T(128)S(6)} %select_n.147, s32[]{:T(128)S(6)} %select_n.146), kind=kLoop, calls=%fused_computation.71 | loop fusion | bytes 1572872 | tf_op jit(solution)/shard_map/jit(dynamic_index_in_dim)/dynamic_slice | solution.py:62
  198.5 2.6 %fusion.31 = f32[384,2048]{1,0:T(8,128)S(1)} fusion(bf16[512,2048]{1,0:T(8,128)(2,1)} %reshape_reshape.16, bf16[384,1,512]{2,0,1:T(8,128)(2,1)S(1)} %copy.75), kind=kOutput, calls=%fused_computation.60 | convolution fusion | flops 805306368 | bytes 5636096 | tf_op jit(solution)/shard_map/dot_general | solution.py:69
  201.0 2.2 %copy.76 = bf16[384,1,512]{2,0,1:T(8,128)(2,1)S(1)} copy(bf16[384,1,512]{0,1,2:T(2,128)(2,1)} %get-tuple-element.27) | data formatting | bytes 786432 | tf_op jit(solution)/shard_map/jit(dynamic_index_in_dim)/dynamic_slice | solution.py:62
  203.2 3.7 %fusion.4 = bf16[1,384,2048]{2,1,0:T(8,128)(2,1)} fusion(f32[384,2048]{1,0:T(8,128)S(1)} %fusion.31, bf16[512,2048]{1,0:T(8,128)(2,1)} %reshape_reshape.13, bf16[384,1,512]{2,0,1:T(8,128)(2,1)S(1)} %copy.76), kind=kOutput, calls=%fused_computation.13 | convolution fusion | flops 806879232 | bytes 7208960 | tf_op jit(solution)/shard_map/dot_general | solution.py:71
  (62 shorter events, 17.7 us)
Async XLA Ops:
  2.4 27.0 %all-to-all-start = ((bf16[8,8,4096]{2,1,0:T(8,128)(2,1)}), bf16[8,8,4096]{2,1,0:T(8,128)(2,1)S(1)}, u32[]{:S(2)}, u32[]{:S(2)}) async-start(bf16[8,8,4096]{2,1,0:T(8,128)(2,1)} %broadcast_in_dim.80), calls=%async_computation | async-start | bytes 1048576 | tf_op jit(solution)/shard_map/all_to_all | solution.py:110
  29.4 8.8 %collective-permute-start.7 = (bf16[8,8,2048]{2,1,0:T(8,128)(2,1)S(1)}, bf16[8,8,2048]{2,1,0:T(8,128)(2,1)S(1)}, u32[]{:S(2)}, u32[]{:S(2)}) collective-permute-start(bf16[8,8,2048]{2,1,0:T(8,128)(2,1)S(1)} %get-tuple-element.29), channel_id=1, source_target_pairs={{0,32},{32,64},{64,96},{96,0},{1,33},{33,65},{65,97},{97,1},{2,34}... | collective-permute-start | bytes 786440 | tf_op jit(solution)/shard_map/ppermute | solution.py:24
  30.7 9.8 %collective-permute-start.8 = (bf16[8,8,2048]{2,1,0:T(8,128)(2,1)S(1)}, bf16[8,8,2048]{2,1,0:T(8,128)(2,1)S(1)}, u32[]{:S(2)}, u32[]{:S(2)}) collective-permute-start(bf16[8,8,2048]{2,1,0:T(8,128)(2,1)S(1)} %get-tuple-element.29), channel_id=1, source_target_pairs={{0,96},{32,0},{64,32},{96,64},{1,97},{33,1},{65,33},{97,65},{2,98}... | collective-permute-start | bytes 786440 | tf_op jit(solution)/shard_map/ppermute | solution.py:27
  32.3 8.2 %collective-permute-start = (bf16[8,8,2048]{2,1,0:T(8,128)(2,1)S(1)}, bf16[8,8,2048]{2,1,0:T(8,128)(2,1)S(1)}, u32[]{:S(2)}, u32[]{:S(2)}) collective-permute-start(bf16[8,8,2048]{2,1,0:T(8,128)(2,1)S(1)} %get-tuple-element.30), channel_id=1, source_target_pairs={{0,16},{16,128},{128,144},{144,0},{1,17},{17,129},{129,145},{145,1... | collective-permute-start | bytes 786440 | tf_op jit(solution)/shard_map/ppermute | solution.py:24
  33.5 7.1 %collective-permute-start.1 = (bf16[8,8,2048]{2,1,0:T(8,128)(2,1)S(1)}, bf16[8,8,2048]{2,1,0:T(8,128)(2,1)S(1)}, u32[]{:S(2)}, u32[]{:S(2)}) collective-permute-start(bf16[8,8,2048]{2,1,0:T(8,128)(2,1)S(1)} %get-tuple-element.30), channel_id=1, source_target_pairs={{0,144},{16,0},{128,16},{144,128},{1,145},{17,1},{129,17},{145,129... | collective-permute-start | bytes 786440 | tf_op jit(solution)/shard_map/ppermute | solution.py:27
  38.1 7.8 %collective-permute-start.9 = (bf16[8,8,2048]{2,1,0:T(8,128)(2,1)S(1)}, bf16[8,8,2048]{2,1,0:T(8,128)(2,1)S(1)}, u32[]{:S(2)}, u32[]{:S(2)}) collective-permute-start(bf16[8,8,2048]{2,1,0:T(8,128)(2,1)S(1)} %collective-permute-done.7), channel_id=1, source_target_pairs={{0,32},{32,64},{64,96},{96,0},{1,33},{33,65},{65,97},{97,1},{2,34}... | collective-permute-start | bytes 786440 | tf_op jit(solution)/shard_map/ppermute | solution.py:24
  40.4 8.3 %collective-permute-start.2 = (bf16[8,8,2048]{2,1,0:T(8,128)(2,1)S(1)}, bf16[8,8,2048]{2,1,0:T(8,128)(2,1)S(1)}, u32[]{:S(2)}, u32[]{:S(2)}) collective-permute-start(bf16[8,8,2048]{2,1,0:T(8,128)(2,1)S(1)} %collective-permute-done), channel_id=1, source_target_pairs={{0,16},{16,128},{128,144},{144,0},{1,17},{17,129},{129,145},{145,1... | collective-permute-start | bytes 786440 | tf_op jit(solution)/shard_map/ppermute | solution.py:24
  46.0 23.9 %collective-permute-start.10 = (bf16[4,8,8,2048]{3,2,1,0:T(8,128)(2,1)S(1)}, bf16[4,8,8,2048]{3,2,1,0:T(8,128)(2,1)S(1)}, u32[]{:S(2)}, u32[]{:S(2)}) collective-permute-start(bf16[4,8,8,2048]{3,2,1,0:T(8,128)(2,1)S(1)} %bitcast_dynamic-update-slice_fusion.8), channel_id=1, source_target_pairs={{0,16},{16,128},{128,144},{144,0},{1,17},{17,129},{129,145},{145,1... | collective-permute-start | bytes 3145736 | tf_op jit(solution)/shard_map/ppermute | solution.py:24
  47.2 25.9 %collective-permute-start.11 = (bf16[4,8,8,2048]{3,2,1,0:T(8,128)(2,1)S(1)}, bf16[4,8,8,2048]{3,2,1,0:T(8,128)(2,1)S(1)}, u32[]{:S(2)}, u32[]{:S(2)}) collective-permute-start(bf16[4,8,8,2048]{3,2,1,0:T(8,128)(2,1)S(1)} %bitcast_dynamic-update-slice_fusion.8), channel_id=1, source_target_pairs={{0,144},{16,0},{128,16},{144,128},{1,145},{17,1},{129,17},{145,129... | collective-permute-start | bytes 3145736 | tf_op jit(solution)/shard_map/ppermute | solution.py:27
  48.7 23.3 %collective-permute-start.3 = (bf16[4,8,8,2048]{3,2,1,0:T(8,128)(2,1)S(1)}, bf16[4,8,8,2048]{3,2,1,0:T(8,128)(2,1)S(1)}, u32[]{:S(2)}, u32[]{:S(2)}) collective-permute-start(bf16[4,8,8,2048]{3,2,1,0:T(8,128)(2,1)S(1)} %bitcast_dynamic-update-slice_fusion.12), channel_id=1, source_target_pairs={{0,32},{32,64},{64,96},{96,0},{1,33},{33,65},{65,97},{97,1},{2,34}... | collective-permute-start | bytes 3145736 | tf_op jit(solution)/shard_map/ppermute | solution.py:24
  48.8 25.4 %collective-permute-start.4 = (bf16[4,8,8,2048]{3,2,1,0:T(8,128)(2,1)S(1)}, bf16[4,8,8,2048]{3,2,1,0:T(8,128)(2,1)S(1)}, u32[]{:S(2)}, u32[]{:S(2)}) collective-permute-start(bf16[4,8,8,2048]{3,2,1,0:T(8,128)(2,1)S(1)} %bitcast_dynamic-update-slice_fusion.12), channel_id=1, source_target_pairs={{0,96},{32,0},{64,32},{96,64},{1,97},{33,1},{65,33},{97,65},{2,98}... | collective-permute-start | bytes 3145736 | tf_op jit(solution)/shard_map/ppermute | solution.py:27
  69.9 22.9 %collective-permute-start.12 = (bf16[4,8,8,2048]{3,2,1,0:T(8,128)(2,1)S(1)}, bf16[4,8,8,2048]{3,2,1,0:T(8,128)(2,1)S(1)}, u32[]{:S(2)}, u32[]{:S(2)}) collective-permute-start(bf16[4,8,8,2048]{3,2,1,0:T(8,128)(2,1)S(1)} %collective-permute-done.10), channel_id=1, source_target_pairs={{0,16},{16,128},{128,144},{144,0},{1,17},{17,129},{129,145},{145,1... | collective-permute-start | bytes 3145736 | tf_op jit(solution)/shard_map/ppermute | solution.py:24
  72.0 25.7 %collective-permute-start.5 = (bf16[4,8,8,2048]{3,2,1,0:T(8,128)(2,1)S(1)}, bf16[4,8,8,2048]{3,2,1,0:T(8,128)(2,1)S(1)}, u32[]{:S(2)}, u32[]{:S(2)}) collective-permute-start(bf16[4,8,8,2048]{3,2,1,0:T(8,128)(2,1)S(1)} %collective-permute-done.3), channel_id=1, source_target_pairs={{0,32},{32,64},{64,96},{96,0},{1,33},{33,65},{65,97},{97,1},{2,34}... | collective-permute-start | bytes 3145736 | tf_op jit(solution)/shard_map/ppermute | solution.py:24
  75.2 24.7 %copy-start.2 = (bf16[1,384,2048]{2,1,0:T(8,128)(2,1)S(1)}, bf16[1,384,2048]{2,1,0:T(8,128)(2,1)}, u32[]{:S(2)}) copy-start(bf16[1,384,2048]{2,1,0:T(8,128)(2,1)} %param.3) | copy-start | bytes 4718596
  93.8 17.9 %collective-permute-start.13 = (bf16[4,4,8,8,2048]{4,3,2,1,0:T(8,128)(2,1)}, bf16[4,4,8,8,2048]{4,3,2,1,0:T(8,128)(2,1)}, u32[]{:S(2)}, u32[]{:S(2)}) collective-permute-start(bf16[4,4,8,8,2048]{4,3,2,1,0:T(8,128)(2,1)} %bitcast_dynamic-update-slice_fusion), channel_id=1, source_target_pairs={{0,1},{1,0},{2,3},{3,2},{4,5},{5,4},{6,7},{7,6},{8,9},{9,8},{10,11... | collective-permute-start | bytes 12582920 | tf_op jit(solution)/shard_map/ppermute | solution.py:44
  98.8 13.0 %collective-permute-start.6 = (bf16[4,4,8,8,2048]{4,3,2,1,0:T(8,128)(2,1)}, bf16[4,4,8,8,2048]{4,3,2,1,0:T(8,128)(2,1)}, u32[]{:S(2)}, u32[]{:S(2)}) collective-permute-start(bf16[4,4,8,8,2048]{4,3,2,1,0:T(8,128)(2,1)} %bitcast_dynamic-update-slice_fusion.4), channel_id=1, source_target_pairs={{0,1},{1,0},{2,3},{3,2},{4,5},{5,4},{6,7},{7,6},{8,9},{9,8},{10,11... | collective-permute-start | bytes 12582920 | tf_op jit(solution)/shard_map/ppermute | solution.py:44
  102.5 4.2 %copy-start.1 = (bf16[384,2,4,2,2,8,8]{0,6,5,4,3,2,1:T(8,128)(2,1)S(1)}, bf16[384,2,4,2,2,8,8]{0,6,5,4,3,2,1:T(8,128)(2,1)}, u32[]{:S(2)}) copy-start(bf16[384,2,4,2,2,8,8]{0,6,5,4,3,2,1:T(8,128)(2,1)} %copy.56) | copy-start | bytes 4718596
  133.2 33.3 %all-to-all-start.1 = ((bf16[1,4,96,4,384]{4,1,3,0,2:T(4,128)(2,1)}), bf16[1,4,96,4,384]{4,1,3,0,2:T(4,128)(2,1)S(1)}, u32[]{:S(2)}, u32[]{:S(2)}) async-start(bf16[1,4,96,4,384]{4,1,3,0,2:T(4,128)(2,1)} %copy.61), calls=%async_computation.1 | async-start | bytes 2359296 | tf_op jit(solution)/shard_map/all_to_all | solution.py:132
  167.4 0.9 copy-start.4
  169.2 9.8 %copy-start = (bf16[4,4,8,8,1024]{4,3,2,1,0:T(8,128)(2,1)S(1)}, bf16[4,4,8,8,1024]{4,3,2,1,0:T(8,128)(2,1)}, u32[]{:S(2)}) copy-start(bf16[4,4,8,8,1024]{4,3,2,1,0:T(8,128)(2,1)} %get-tuple-element.22) | copy-start | bytes 6291460
  173.4 19.7 %all-to-all-start.2 = ((bf16[1,128,3,4,128]{4,3,2,0,1:T(4,128)(2,1)}), bf16[1,128,3,4,128]{4,3,2,0,1:T(4,128)(2,1)S(1)}, u32[]{:S(2)}, u32[]{:S(2)}) async-start(bf16[1,128,3,4,128]{4,3,2,0,1:T(4,128)(2,1)} %bitcast.46), calls=%async_computation.2 | async-start | bytes 786432 | tf_op jit(solution)/shard_map/all_to_all | solution.py:100
  181.2 12.3 %copy-start.3 = (bf16[1,4,384,128]{3,2,1,0:T(8,128)(2,1)S(1)}, bf16[1,4,384,128]{3,2,1,0:T(8,128)(2,1)}, u32[]{:S(2)}) copy-start(bf16[1,4,384,128]{3,2,1,0:T(8,128)(2,1)} %fusion.5) | copy-start | bytes 1179652

commit v2 on v1

--- a/solution.py
+++ b/solution.py
@@ -112,16 +112,19 @@
     spare = both.shape[1] - w_qkv.shape[1]
     pieces, tail = [], None
     for p, axes in enumerate(PARTS):
-        own, other = with_other(rings(along_z[..., p * step:(p + 1) * step], axes))
+        own = rings(along_z[..., p * step:(p + 1) * step], axes)
         order = order_of(("z",) + axes)
         if p == len(PARTS) - 1:
             width = step - spare
-            tail = (own[..., width:], other[..., width:]), order
-            own, other = own[..., :width], other[..., :width]
+            tail = own[..., width:], order
+            own = own[..., :width]
+        own, other = with_other(own)
         gathered = flat_rows((own, other), own.shape[-1])
         pieces.append(project(flat, w_qkv.shape[0], gathered, order))
     qkv = jnp.concatenate(pieces, axis=1).astype(jnp.bfloat16)
-    (out_own, out_other), out_order = tail
+    out_own, out_order = tail
+    out_own, qkv = lax.optimization_barrier((out_own, qkv))
+    out_own, out_other = with_other(out_own)
     lead = out_own.shape[:-2]
     out_w = tuple(
         a.reshape(*lead, w_out.shape[0], w_out.shape[1]).reshape(-1, w_out.shape[1])

time: 208 us -> 208 us (level)
  local copies, waits for them, and re-layouts: 54.7 us -> 49.3 us
  matrix products: 24.1 us -> 27.1 us
  waiting for transfers between devices: 88.4 us -> 91.2 us
    slice x3 -> x2, local copies, waits for them, and re-layouts: 8.44 us -> 2.53 us  [the longest x1 2.49 us: on_device(): own = own[..., :width]]
    ppermute x8, waiting for transfers between devices: 40.4 us -> 45.7 us  [ring(): fwd = lax.ppermute(fwd, axis, [(i, (i + 1) % n) for i in range(n)])]
    concatenate x1 -> x0, local copies, waits for them, and re-layouts: 3 us -> none  [on_device(): qkv = jnp.concatenate(pieces, axis=1).astype(jnp.bfloat16)]
    reshape x2, local copies, waits for them, and re-layouts: 0.91 us -> 3.65 us  [column_heads(): flat = packed.reshape(seq_count, length, count, 3, width // 3)]
    all_to_all x1, waiting for transfers between devices: 22.2 us -> 19.8 us  [on_device(): lax.all_to_all(col_packed, SEQ, split_axis=2, concat_axis=1, tiled=True)]
    optimization_barrier x0 -> x1, local copies, waits for them, and re-layouts: none -> 2.44 us  [on_device(): out_own, qkv = lax.optimization_barrier((out_own, qkv))]
    ppermute x2 -> x3, starting transfers between devices: 4.97 us -> 4.5 us  [with_other(): return (own, lax.ppermute(own, 'c', [(0, 1), (1, 0)]))]
  transfers between devices with their start and end apart: 17 -> 18, of which waited for: 9 -> 10; matrix products, arithmetic and copies ran while one was open for 19% -> 23% of each run, Pallas kernels for 0% -> 0%
where the time goes in v2:
time: 208 us; the launch traced here: 207 us
  waiting for transfers between devices  91.2 us (44%)
  local copies, waits for them, and re-layouts  49.3 us (24%)
  starting transfers between devices  34.7 us (17%)
  matrix products  27.1 us (13%)
  other arithmetic  4.56 us (2%)
    ppermute x8, waiting for transfers between devices, ring(): fwd = lax.ppermute(fwd, axis, [(i, (i + 1) % n) for i in range(n)])  45.7 us
    all_to_all x1, waiting for transfers between devices, on_device(): lax.all_to_all(col_packed, SEQ, split_axis=2, concat_axis=1, tiled=True)  19.8 us
    all_to_all x1, waiting for transfers between devices, on_device(): along_z = lax.all_to_all(spread, 'z', 0, 0, tiled=True)  18 us
    dot_general x3, matrix products, project(): first = jnp.dot(own, own_w, preferred_element_type=jnp.float32)  9.54 us
    dot_general x3, matrix products, project(): return first + jnp.dot(other, other_w, preferred_element_type=jnp.float32)  9.21 us
    all_to_all x1, starting transfers between devices, on_device(): along_z = lax.all_to_all(spread, 'z', 0, 0, tiled=True)  9 us
    all_to_all x1, waiting for transfers between devices, column_heads(): return lax.all_to_all(result, SEQ, split_axis=1, concat_axis=2, tiled=True)  7.76 us
    ppermute x4, starting transfers between devices, ring(): bwd = lax.ppermute(bwd, axis, [(i, (i - 1) % n) for i in range(n)])  6.66 us
  transfers between devices with their start and end apart: 18, of which 10 were waited for; matrix products, arithmetic and copies ran while one was open for 23% of the time, Pallas kernels for 0%

profile of v2, /device:TPU:1, one launch (start us, length us, event | category | flops | bytes accessed | tf_op | source)
XLA Modules:
  0.0 207.2 jit_solution(15695047766224345039)
XLA Ops:
  2.4 9.0 %all-to-all-start = ((bf16[8,8,4096]{2,1,0:T(8,128)(2,1)}), bf16[8,8,4096]{2,1,0:T(8,128)(2,1)S(1)}, u32[]{:S(2)}, u32[]{:S(2)}) async-start(bf16[8,8,4096]{2,1,0:T(8,128)(2,1)} %broadcast_in_dim.80), calls=%async_computation | async-start | bytes 1048576 | tf_op jit(solution)/shard_map/all_to_all | solution.py:110
  11.4 18.0 %all-to-all-done = bf16[8,8,4096]{2,1,0:T(8,128)(2,1)S(1)} async-done(((bf16[8,8,4096]{2,1,0:T(8,128)(2,1)}), bf16[8,8,4096]{2,1,0:T(8,128)(2,1)S(1)}, u32[]{:S(2)}, u32[]{:S(2)}) %all-to-all-start) | async-done | bytes 524320 | tf_op jit(solution)/shard_map/all_to_all | solution.py:110
  29.4 1.4 collective-permute-start.6
  30.7 1.5 collective-permute-start.7
  32.3 1.2 collective-permute-start
  33.5 1.5 collective-permute-start.1
  35.2 2.9 %collective-permute-done.6 = bf16[8,8,2048]{2,1,0:T(8,128)(2,1)S(1)} collective-permute-done((bf16[8,8,2048]{2,1,0:T(8,128)(2,1)S(1)}, bf16[8,8,2048]{2,1,0:T(8,128)(2,1)S(1)}, u32[]{:S(2)}, u32[]{:S(2)}) %collective-permute-start.6) | collective-permute-done | bytes 262176 | tf_op jit(solution)/shard_map/ppermute | solution.py:24
  38.2 2.3 %collective-permute-done = bf16[8,8,2048]{2,1,0:T(8,128)(2,1)S(1)} collective-permute-done((bf16[8,8,2048]{2,1,0:T(8,128)(2,1)S(1)}, bf16[8,8,2048]{2,1,0:T(8,128)(2,1)S(1)}, u32[]{:S(2)}, u32[]{:S(2)}) %collective-permute-start) | collective-permute-done | bytes 262176 | tf_op jit(solution)/shard_map/ppermute | solution.py:24
  40.5 5.4 %collective-permute-done.8 = bf16[8,8,2048]{2,1,0:T(8,128)(2,1)S(1)} collective-permute-done((bf16[8,8,2048]{2,1,0:T(8,128)(2,1)S(1)}, bf16[8,8,2048]{2,1,0:T(8,128)(2,1)S(1)}, u32[]{:S(2)}, u32[]{:S(2)}) %collective-permute-start.8) | collective-permute-done | bytes 262176 | tf_op jit(solution)/shard_map/ppermute | solution.py:24
  46.0 1.3 collective-permute-start.9
  47.9 1.1 collective-permute-start.10
  49.0 2.6 %collective-permute-start.4 = (bf16[4,8,8,2048]{3,2,1,0:T(8,128)(2,1)S(1)}, bf16[4,8,8,2048]{3,2,1,0:T(8,128)(2,1)S(1)}, u32[]{:S(2)}, u32[]{:S(2)}) collective-permute-start(bf16[4,8,8,2048]{3,2,1,0:T(8,128)(2,1)S(1)} %bitcast_dynamic-update-slice_fusion.12), channel_id=1, source_target_pairs={{0,96},{32,0},{64,32},{96,64},{1,97},{33,1},{65,33},{97,65},{2,98}... | collective-permute-start | bytes 3145736 | tf_op jit(solution)/shard_map/ppermute | solution.py:27
  51.5 2.5 %broadcast.134.clone.1 = bf16[4,4,8,8,2048]{4,3,2,1,0:T(8,128)(2,1)} broadcast(bf16[]{:T(256)} %constant.153.clone.1), dimensions={} | broadcast | bytes 4194306 | tf_op jit(solution)/shard_map/broadcast.8
  54.0 1.0 bitcast_dynamic-update-slice_fusion.3
  55.1 14.8 %collective-permute-done.9 = bf16[4,8,8,2048]{3,2,1,0:T(8,128)(2,1)S(1)} collective-permute-done((bf16[4,8,8,2048]{3,2,1,0:T(8,128)(2,1)S(1)}, bf16[4,8,8,2048]{3,2,1,0:T(8,128)(2,1)S(1)}, u32[]{:S(2)}, u32[]{:S(2)}) %collective-permute-start.9) | collective-permute-done | bytes 1048608 | tf_op jit(solution)/shard_map/ppermute | solution.py:24
  71.4 1.1 bitcast_dynamic-update-slice_fusion.2
  72.5 1.1 bitcast_dynamic-update-slice_fusion.1
  73.6 19.2 %collective-permute-done.11 = bf16[4,8,8,2048]{3,2,1,0:T(8,128)(2,1)S(1)} collective-permute-done((bf16[4,8,8,2048]{3,2,1,0:T(8,128)(2,1)S(1)}, bf16[4,8,8,2048]{3,2,1,0:T(8,128)(2,1)S(1)}, u32[]{:S(2)}, u32[]{:S(2)}) %collective-permute-start.11) | collective-permute-done | bytes 1048608 | tf_op jit(solution)/shard_map/ppermute | solution.py:24
  92.8 1.1 bitcast_dynamic-update-slice_fusion
  93.9 3.8 %collective-permute-start.12 = (bf16[4,4,8,8,2048]{4,3,2,1,0:T(8,128)(2,1)}, bf16[4,4,8,8,2048]{4,3,2,1,0:T(8,128)(2,1)}, u32[]{:S(2)}, u32[]{:S(2)}) collective-permute-start(bf16[4,4,8,8,2048]{4,3,2,1,0:T(8,128)(2,1)} %bitcast_dynamic-update-slice_fusion), channel_id=1, source_target_pairs={{0,1},{1,0},{2,3},{3,2},{4,5},{5,4},{6,7},{7,6},{8,9},{9,8},{10,11... | collective-permute-start | bytes 12582920 | tf_op jit(solution)/shard_map/ppermute | solution.py:44
  98.2 2.5 %fusion.55 = (bf16[4,4,8,8,1024]{4,3,2,1,0:T(8,128)(2,1)}, bf16[4,4,8,8,1024]{4,3,2,1,0:T(8,128)(2,1)}) fusion(bf16[4,4,8,8,2048]{4,3,2,1,0:T(8,128)(2,1)S(1)} %bitcast_dynamic-update-slice_fusion.4), kind=kLoop, calls=%fused_computation.97 | loop fusion | bytes 8388608 | tf_op jit(solution)/shard_map/slice | solution.py:120
  101.8 1.4 copy.56
  103.2 2.8 %fusion.15 = f32[384,1024]{1,0:T(8,128)S(1)} fusion(bf16[1024,1024]{1,0:T(8,128)(2,1)} %bitcast.27, bf16[384,2,1024]{0,2,1:T(8,128)(2,1)} %bitcast.182, s32[]{:T(128)S(6)} %select_n.146), kind=kOutput, calls=%fused_computation.37 | convolution fusion | flops 805306368 | bytes 4456452 | tf_op jit(solution)/shard_map/dot_general | solution.py:69
  106.1 4.1 %fusion.19 = f32[384,2048]{1,0:T(8,128)S(1)} fusion(bf16[1024,2048]{1,0:T(8,128)(2,1)} %bitcast.21, bf16[384,2,1024]{0,2,1:T(8,128)(2,1)S(1)} %bitcast.180, s32[]{:T(128)S(6)} %select_n.146), kind=kOutput, calls=%fused_computation.41 | convolution fusion | flops 1610612736 | bytes 8126468 | tf_op jit(solution)/shard_map/dot_general | solution.py:69
  110.2 2.6 %fusion.13 = f32[384,1024]{1,0:T(8,128)S(1)} fusion(bf16[1024,1024]{1,0:T(8,128)(2,1)} %bitcast.23, bf16[384,2,1024]{0,2,1:T(8,128)(2,1)S(1)} %bitcast.183, s32[]{:T(128)S(6)} %select_n.147), kind=kOutput, calls=%fused_computation.35 | convolution fusion | flops 805306368 | bytes 4456452 | tf_op jit(solution)/shard_map/dot_general | solution.py:71
  113.2 4.0 %fusion.17 = f32[384,2048]{1,0:T(8,128)S(1)} fusion(bf16[1024,2048]{1,0:T(8,128)(2,1)} %bitcast.16, bf16[384,2,1024]{0,2,1:T(8,128)(2,1)S(1)} %bitcast.181, s32[]{:T(128)S(6)} %select_n.147), kind=kOutput, calls=%fused_computation.39 | convolution fusion | flops 1610612736 | bytes 8126468 | tf_op jit(solution)/shard_map/dot_general | solution.py:71
  118.1 2.4 %copy.59 = bf16[384,3072]{0,1:T(8,128)(2,1)} copy(bf16[384,3072]{1,0:T(8,128)(2,1)S(1)} %pad_maximum_fusion) | data formatting | bytes 4718592 | tf_op jit(solution)/shard_map/optimization_barrier | solution.py:126
  120.6 3.0 %fusion.56 = (bf16[1,384,4,3,128]{1,4,3,2,0:T(8,128)(2,1)}, bf16[1,384,4,3,128]{1,4,3,2,0:T(8,128)(2,1)S(1)}) fusion(bf16[1,384,8,3,128]{1,4,3,2,0:T(8,128)(2,1)} %bitcast.178), kind=kLoop, calls=%fused_computation.98 | loop fusion | bytes 4718592 | tf_op jit(solution)/shard_map/slice | solution.py:136
  123.6 2.1 reshape.206
  125.6 4.3 %copy.61 = bf16[1,4,96,4,384]{4,1,3,0,2:T(4,128)(2,1)} copy(bf16[1,4,96,4,384]{2,1,4,3,0:T(4,128)(2,1)} %reshape.206) | data formatting | bytes 2359296 | tf_op jit(solution)/shard_map/reshape | solution.py:134
  129.9 4.1 %all-to-all-start.1 = ((bf16[1,4,96,4,384]{4,1,3,0,2:T(4,128)(2,1)}), bf16[1,4,96,4,384]{4,1,3,0,2:T(4,128)(2,1)S(1)}, u32[]{:S(2)}, u32[]{:S(2)}) async-start(bf16[1,4,96,4,384]{4,1,3,0,2:T(4,128)(2,1)} %copy.61), calls=%async_computation.1 | async-start | bytes 2359296 | tf_op jit(solution)/shard_map/all_to_all | solution.py:135
  135.6 2.4 %copy.81 = bf16[1,384,4,3,128]{4,1,2,3,0:T(8,128)(2,1)} copy(bf16[1,384,4,3,128]{1,4,3,2,0:T(8,128)(2,1)} %get-tuple-element.27) | data formatting | bytes 2359296
  138.0 2.1 fusion.58
  140.1 3.3 %fusion.5 = bf16[1,4,384,128]{3,2,1,0:T(8,128)(2,1)} fusion(f32[4,384]{1,0:T(4,128)S(1)} %fusion.58, bf16[1,4,3,384,128]{4,3,1,2,0:T(8,128)(2,1)} %bitcast.190, pred[384,384]{0,1:T(8,128)(4,1)} %fusion.26), kind=kOutput, calls=%fused_computation.17 | convolution fusion | flops 305137536 | bytes 1726464 | tf_op jit(solution)/shard_map/shqk,shkd->shqd/dot_general | solution.py:82
  143.4 19.8 %all-to-all-done.1 = bf16[1,4,96,4,384]{4,1,3,0,2:T(4,128)(2,1)S(1)} async-done(((bf16[1,4,96,4,384]{4,1,3,0,2:T(4,128)(2,1)}), bf16[1,4,96,4,384]{4,1,3,0,2:T(4,128)(2,1)S(1)}, u32[]{:S(2)}, u32[]{:S(2)}) %all-to-all-start.1) | async-done | bytes 1179680 | tf_op jit(solution)/shard_map/all_to_all | solution.py:135
  164.0 1.9 reshape.198
  165.9 1.8 copy.83
  168.6 2.1 fusion.6
  170.6 2.1 copy.68
  172.7 6.2 %all-to-all-start.2 = ((bf16[1,128,3,4,128]{4,3,2,0,1:T(4,128)(2,1)}), bf16[1,128,3,4,128]{4,3,2,0,1:T(4,128)(2,1)S(1)}, u32[]{:S(2)}, u32[]{:S(2)}) async-start(bf16[1,128,3,4,128]{4,3,2,0,1:T(4,128)(2,1)} %bitcast.46), calls=%async_computation.2 | async-start | bytes 786432 | tf_op jit(solution)/shard_map/all_to_all | solution.py:100
  178.9 2.2 %reshape_reshape.16 = bf16[512,2048]{1,0:T(8,128)(2,1)} reshape(bf16[4,4,8,8,1024]{4,3,2,1,0:T(8,128)(2,1)S(1)} %copy-done) | data formatting | bytes 4194304 | tf_op jit(solution)/shard_map/reshape;reshape | solution.py:130
  181.1 4.1 %reshape_reshape.14 = bf16[512,2048]{1,0:T(8,128)(2,1)} reshape(bf16[4,4,8,8,1024]{4,3,2,1,0:T(8,128)(2,1)} %collective-permute-done.14) | data formatting | bytes 4194304 | tf_op jit(solution)/shard_map/reshape;reshape | solution.py:130
  185.2 7.8 %all-to-all-done.2 = bf16[1,128,3,4,128]{4,3,2,0,1:T(4,128)(2,1)S(1)} async-done(((bf16[1,128,3,4,128]{4,3,2,0,1:T(4,128)(2,1)}), bf16[1,128,3,4,128]{4,3,2,0,1:T(4,128)(2,1)S(1)}, u32[]{:S(2)}, u32[]{:S(2)}) %all-to-all-start.2) | async-done | bytes 393248 | tf_op jit(solution)/shard_map/all_to_all | solution.py:100
  194.9 2.5 %constant_dynamic-slice_fusion = (bf16[384,1,512]{0,1,2:T(2,128)(2,1)}, bf16[384,1,512]{0,1,2:T(2,128)(2,1)S(1)}) fusion(bf16[384,2,512]{0,1,2:T(2,128)(2,1)S(1)} %bitcast.179, s32[]{:T(128)S(6)} %select_n.147, s32[]{:T(128)S(6)} %select_n.146), kind=kLoop, calls=%fused_computation.71 | loop fusion | bytes 1572872 | tf_op jit(solution)/shard_map/jit(dynamic_index_in_dim)/dynamic_slice | solution.py:62
  198.4 2.6 %fusion.31 = f32[384,2048]{1,0:T(8,128)S(1)} fusion(bf16[512,2048]{1,0:T(8,128)(2,1)} %reshape_reshape.16, bf16[384,1,512]{2,0,1:T(8,128)(2,1)S(1)} %copy.75), kind=kOutput, calls=%fused_computation.60 | convolution fusion | flops 805306368 | bytes 5636096 | tf_op jit(solution)/shard_map/dot_general | solution.py:69
  200.9 2.2 %copy.76 = bf16[384,1,512]{2,0,1:T(8,128)(2,1)S(1)} copy(bf16[384,1,512]{0,1,2:T(2,128)(2,1)} %get-tuple-element.29) | data formatting | bytes 786432 | tf_op jit(solution)/shard_map/jit(dynamic_index_in_dim)/dynamic_slice | solution.py:62
  203.1 2.6 %fusion.29 = f32[384,2048]{1,0:T(8,128)S(1)} fusion(bf16[512,2048]{1,0:T(8,128)(2,1)} %reshape_reshape.14, bf16[384,1,512]{2,0,1:T(8,128)(2,1)S(1)} %copy.76), kind=kOutput, calls=%fused_computation.58 | convolution fusion | flops 805306368 | bytes 5636096 | tf_op jit(solution)/shard_map/dot_general | solution.py:71
  205.7 1.5 fusion.4
  (63 shorter events, 13.8 us)
Async XLA Ops:
  2.4 27.0 %all-to-all-start = ((bf16[8,8,4096]{2,1,0:T(8,128)(2,1)}), bf16[8,8,4096]{2,1,0:T(8,128)(2,1)S(1)}, u32[]{:S(2)}, u32[]{:S(2)}) async-start(bf16[8,8,4096]{2,1,0:T(8,128)(2,1)} %broadcast_in_dim.80), calls=%async_computation | async-start | bytes 1048576 | tf_op jit(solution)/shard_map/all_to_all | solution.py:110
  29.4 8.8 %collective-permute-start.6 = (bf16[8,8,2048]{2,1,0:T(8,128)(2,1)S(1)}, bf16[8,8,2048]{2,1,0:T(8,128)(2,1)S(1)}, u32[]{:S(2)}, u32[]{:S(2)}) collective-permute-start(bf16[8,8,2048]{2,1,0:T(8,128)(2,1)S(1)} %get-tuple-element.31), channel_id=1, source_target_pairs={{0,32},{32,64},{64,96},{96,0},{1,33},{33,65},{65,97},{97,1},{2,34}... | collective-permute-start | bytes 786440 | tf_op jit(solution)/shard_map/ppermute | solution.py:24
  30.7 9.8 %collective-permute-start.7 = (bf16[8,8,2048]{2,1,0:T(8,128)(2,1)S(1)}, bf16[8,8,2048]{2,1,0:T(8,128)(2,1)S(1)}, u32[]{:S(2)}, u32[]{:S(2)}) collective-permute-start(bf16[8,8,2048]{2,1,0:T(8,128)(2,1)S(1)} %get-tuple-element.31), channel_id=1, source_target_pairs={{0,96},{32,0},{64,32},{96,64},{1,97},{33,1},{65,33},{97,65},{2,98}... | collective-permute-start | bytes 786440 | tf_op jit(solution)/shard_map/ppermute | solution.py:27
  32.3 8.2 %collective-permute-start = (bf16[8,8,2048]{2,1,0:T(8,128)(2,1)S(1)}, bf16[8,8,2048]{2,1,0:T(8,128)(2,1)S(1)}, u32[]{:S(2)}, u32[]{:S(2)}) collective-permute-start(bf16[8,8,2048]{2,1,0:T(8,128)(2,1)S(1)} %get-tuple-element.32), channel_id=1, source_target_pairs={{0,16},{16,128},{128,144},{144,0},{1,17},{17,129},{129,145},{145,1... | collective-permute-start | bytes 786440 | tf_op jit(solution)/shard_map/ppermute | solution.py:24
  33.5 13.8 %collective-permute-start.1 = (bf16[8,8,2048]{2,1,0:T(8,128)(2,1)S(1)}, bf16[8,8,2048]{2,1,0:T(8,128)(2,1)S(1)}, u32[]{:S(2)}, u32[]{:S(2)}) collective-permute-start(bf16[8,8,2048]{2,1,0:T(8,128)(2,1)S(1)} %get-tuple-element.32), channel_id=1, source_target_pairs={{0,144},{16,0},{128,16},{144,128},{1,145},{17,1},{129,17},{145,129... | collective-permute-start | bytes 786440 | tf_op jit(solution)/shard_map/ppermute | solution.py:27
  38.1 7.8 %collective-permute-start.8 = (bf16[8,8,2048]{2,1,0:T(8,128)(2,1)S(1)}, bf16[8,8,2048]{2,1,0:T(8,128)(2,1)S(1)}, u32[]{:S(2)}, u32[]{:S(2)}) collective-permute-start(bf16[8,8,2048]{2,1,0:T(8,128)(2,1)S(1)} %collective-permute-done.6), channel_id=1, source_target_pairs={{0,32},{32,64},{64,96},{96,0},{1,33},{33,65},{65,97},{97,1},{2,34}... | collective-permute-start | bytes 786440 | tf_op jit(solution)/shard_map/ppermute | solution.py:24
  40.4 7.3 %collective-permute-start.2 = (bf16[8,8,2048]{2,1,0:T(8,128)(2,1)S(1)}, bf16[8,8,2048]{2,1,0:T(8,128)(2,1)S(1)}, u32[]{:S(2)}, u32[]{:S(2)}) collective-permute-start(bf16[8,8,2048]{2,1,0:T(8,128)(2,1)S(1)} %collective-permute-done), channel_id=1, source_target_pairs={{0,16},{16,128},{128,144},{144,0},{1,17},{17,129},{129,145},{145,1... | collective-permute-start | bytes 786440 | tf_op jit(solution)/shard_map/ppermute | solution.py:24
  46.0 23.9 %collective-permute-start.9 = (bf16[4,8,8,2048]{3,2,1,0:T(8,128)(2,1)S(1)}, bf16[4,8,8,2048]{3,2,1,0:T(8,128)(2,1)S(1)}, u32[]{:S(2)}, u32[]{:S(2)}) collective-permute-start(bf16[4,8,8,2048]{3,2,1,0:T(8,128)(2,1)S(1)} %bitcast_dynamic-update-slice_fusion.8), channel_id=1, source_target_pairs={{0,16},{16,128},{128,144},{144,0},{1,17},{17,129},{129,145},{145,1... | collective-permute-start | bytes 3145736 | tf_op jit(solution)/shard_map/ppermute | solution.py:24
  47.8 23.4 %collective-permute-start.3 = (bf16[4,8,8,2048]{3,2,1,0:T(8,128)(2,1)S(1)}, bf16[4,8,8,2048]{3,2,1,0:T(8,128)(2,1)S(1)}, u32[]{:S(2)}, u32[]{:S(2)}) collective-permute-start(bf16[4,8,8,2048]{3,2,1,0:T(8,128)(2,1)S(1)} %bitcast_dynamic-update-slice_fusion.12), channel_id=1, source_target_pairs={{0,32},{32,64},{64,96},{96,0},{1,33},{33,65},{65,97},{97,1},{2,34}... | collective-permute-start | bytes 3145736 | tf_op jit(solution)/shard_map/ppermute | solution.py:24
  47.9 24.6 %collective-permute-start.10 = (bf16[4,8,8,2048]{3,2,1,0:T(8,128)(2,1)S(1)}, bf16[4,8,8,2048]{3,2,1,0:T(8,128)(2,1)S(1)}, u32[]{:S(2)}, u32[]{:S(2)}) collective-permute-start(bf16[4,8,8,2048]{3,2,1,0:T(8,128)(2,1)S(1)} %bitcast_dynamic-update-slice_fusion.8), channel_id=1, source_target_pairs={{0,144},{16,0},{128,16},{144,128},{1,145},{17,1},{129,17},{145,129... | collective-permute-start | bytes 3145736 | tf_op jit(solution)/shard_map/ppermute | solution.py:27
  49.0 48.9 %collective-permute-start.4 = (bf16[4,8,8,2048]{3,2,1,0:T(8,128)(2,1)S(1)}, bf16[4,8,8,2048]{3,2,1,0:T(8,128)(2,1)S(1)}, u32[]{:S(2)}, u32[]{:S(2)}) collective-permute-start(bf16[4,8,8,2048]{3,2,1,0:T(8,128)(2,1)S(1)} %bitcast_dynamic-update-slice_fusion.12), channel_id=1, source_target_pairs={{0,96},{32,0},{64,32},{96,64},{1,97},{33,1},{65,33},{97,65},{2,98}... | collective-permute-start | bytes 3145736 | tf_op jit(solution)/shard_map/ppermute | solution.py:27
  69.9 22.9 %collective-permute-start.11 = (bf16[4,8,8,2048]{3,2,1,0:T(8,128)(2,1)S(1)}, bf16[4,8,8,2048]{3,2,1,0:T(8,128)(2,1)S(1)}, u32[]{:S(2)}, u32[]{:S(2)}) collective-permute-start(bf16[4,8,8,2048]{3,2,1,0:T(8,128)(2,1)S(1)} %collective-permute-done.9), channel_id=1, source_target_pairs={{0,16},{16,128},{128,144},{144,0},{1,17},{17,129},{129,145},{145,1... | collective-permute-start | bytes 3145736 | tf_op jit(solution)/shard_map/ppermute | solution.py:24
  71.2 26.9 %collective-permute-start.5 = (bf16[4,8,8,2048]{3,2,1,0:T(8,128)(2,1)S(1)}, bf16[4,8,8,2048]{3,2,1,0:T(8,128)(2,1)S(1)}, u32[]{:S(2)}, u32[]{:S(2)}) collective-permute-start(bf16[4,8,8,2048]{3,2,1,0:T(8,128)(2,1)S(1)} %collective-permute-done.3), channel_id=1, source_target_pairs={{0,32},{32,64},{64,96},{96,0},{1,33},{33,65},{65,97},{97,1},{2,34}... | collective-permute-start | bytes 3145736 | tf_op jit(solution)/shard_map/ppermute | solution.py:24
  93.9 19.3 %collective-permute-start.12 = (bf16[4,4,8,8,2048]{4,3,2,1,0:T(8,128)(2,1)}, bf16[4,4,8,8,2048]{4,3,2,1,0:T(8,128)(2,1)}, u32[]{:S(2)}, u32[]{:S(2)}) collective-permute-start(bf16[4,4,8,8,2048]{4,3,2,1,0:T(8,128)(2,1)} %bitcast_dynamic-update-slice_fusion), channel_id=1, source_target_pairs={{0,1},{1,0},{2,3},{3,2},{4,5},{5,4},{6,7},{7,6},{8,9},{9,8},{10,11... | collective-permute-start | bytes 12582920 | tf_op jit(solution)/shard_map/ppermute | solution.py:44
  98.1 2.5 %copy-start.2 = (bf16[1,384,2048]{2,1,0:T(8,128)(2,1)S(1)}, bf16[1,384,2048]{2,1,0:T(8,128)(2,1)}, u32[]{:S(2)}) copy-start(bf16[1,384,2048]{2,1,0:T(8,128)(2,1)} %param.3) | copy-start | bytes 4718596
  100.6 9.6 %collective-permute-start.13 = (bf16[4,4,8,8,1024]{4,3,2,1,0:T(8,128)(2,1)}, bf16[4,4,8,8,1024]{4,3,2,1,0:T(8,128)(2,1)}, u32[]{:S(2)}, u32[]{:S(2)}) collective-permute-start(bf16[4,4,8,8,1024]{4,3,2,1,0:T(8,128)(2,1)} %get-tuple-element.25), channel_id=1, source_target_pairs={{0,1},{1,0},{2,3},{3,2},{4,5},{5,4},{6,7},{7,6},{8,9},{9,8},{10,11... | collective-permute-start | bytes 6291464 | tf_op jit(solution)/shard_map/ppermute | solution.py:44
  106.1 4.2 %copy-start.1 = (bf16[384,2,4,2,2,8,8]{0,6,5,4,3,2,1:T(8,128)(2,1)S(1)}, bf16[384,2,4,2,2,8,8]{0,6,5,4,3,2,1:T(8,128)(2,1)}, u32[]{:S(2)}) copy-start(bf16[384,2,4,2,2,8,8]{0,6,5,4,3,2,1:T(8,128)(2,1)} %copy.56) | copy-start | bytes 4718596
  125.6 8.4 %copy-start = (bf16[4,4,8,8,1024]{4,3,2,1,0:T(8,128)(2,1)S(1)}, bf16[4,4,8,8,1024]{4,3,2,1,0:T(8,128)(2,1)}, u32[]{:S(2)}) copy-start(bf16[4,4,8,8,1024]{4,3,2,1,0:T(8,128)(2,1)} %get-tuple-element.19) | copy-start | bytes 6291460
  129.9 33.2 %all-to-all-start.1 = ((bf16[1,4,96,4,384]{4,1,3,0,2:T(4,128)(2,1)}), bf16[1,4,96,4,384]{4,1,3,0,2:T(4,128)(2,1)S(1)}, u32[]{:S(2)}, u32[]{:S(2)}) async-start(bf16[1,4,96,4,384]{4,1,3,0,2:T(4,128)(2,1)} %copy.61), calls=%async_computation.1 | async-start | bytes 2359296 | tf_op jit(solution)/shard_map/all_to_all | solution.py:135
  134.0 47.1 %collective-permute-start.14 = (bf16[4,4,8,8,1024]{4,3,2,1,0:T(8,128)(2,1)S(1)}, bf16[4,4,8,8,1024]{4,3,2,1,0:T(8,128)(2,1)}, u32[]{:S(2)}, u32[]{:S(2)}) collective-permute-start(bf16[4,4,8,8,1024]{4,3,2,1,0:T(8,128)(2,1)S(1)} %copy-done), channel_id=1, source_target_pairs={{0,1},{1,0},{2,3},{3,2},{4,5},{5,4},{6,7},{7,6},{8,9},{9,8},{10,11... | collective-permute-start | bytes 6291464 | tf_op jit(solution)/shard_map/ppermute | solution.py:44
  172.7 20.3 %all-to-all-start.2 = ((bf16[1,128,3,4,128]{4,3,2,0,1:T(4,128)(2,1)}), bf16[1,128,3,4,128]{4,3,2,0,1:T(4,128)(2,1)S(1)}, u32[]{:S(2)}, u32[]{:S(2)}) async-start(bf16[1,128,3,4,128]{4,3,2,0,1:T(4,128)(2,1)} %bitcast.46), calls=%async_computation.2 | async-start | bytes 786432 | tf_op jit(solution)/shard_map/all_to_all | solution.py:100
  181.1 12.3 %copy-start.3 = (bf16[1,4,384,128]{3,2,1,0:T(8,128)(2,1)S(1)}, bf16[1,4,384,128]{3,2,1,0:T(8,128)(2,1)}, u32[]{:S(2)}) copy-start(bf16[1,4,384,128]{3,2,1,0:T(8,128)(2,1)} %fusion.5) | copy-start | bytes 1179652

commit v3 on v1

--- a/solution.py
+++ b/solution.py
@@ -118,19 +118,29 @@
             width = step - spare
             tail = (own[..., width:], other[..., width:]), order
             own, other = own[..., :width], other[..., :width]
-        gathered = flat_rows((own, other), own.shape[-1])
-        pieces.append(project(flat, w_qkv.shape[0], gathered, order))
-    qkv = jnp.concatenate(pieces, axis=1).astype(jnp.bfloat16)
+        pieces.append((flat_rows((own, other), own.shape[-1]), order))
+    split = half * 3 * HEAD_DIM
+    (first_w, first_order), (second_w, second_order) = pieces
+    col_qkv = jnp.concatenate(
+        [
+            project(flat, w_qkv.shape[0], tuple(a[:, split:] for a in first_w), first_order),
+            project(flat, w_qkv.shape[0], second_w, second_order),
+        ],
+        axis=1,
+    ).astype(jnp.bfloat16)
+    row_qkv = project(
+        flat, w_qkv.shape[0], tuple(a[:, :split] for a in first_w), first_order
+    ).astype(jnp.bfloat16)
     (out_own, out_other), out_order = tail
     lead = out_own.shape[:-2]
     out_w = tuple(
         a.reshape(*lead, w_out.shape[0], w_out.shape[1]).reshape(-1, w_out.shape[1])
         for a in (out_own, out_other)
     )
-    qkv = qkv.reshape(seq_count, tok_count, HEADS, 3, HEAD_DIM)
-    col_packed = qkv[:, :, half:].reshape(seq_count, tok_count // COLS, COLS, half, 3 * HEAD_DIM)
+    col_packed = col_qkv.reshape(seq_count, tok_count // COLS, COLS, half, 3 * HEAD_DIM)
     received = lax.all_to_all(col_packed, SEQ, split_axis=2, concat_axis=1, tiled=True)
-    row_part = jnp.transpose(qkv[:, :, :half], (0, 2, 3, 1, 4))
+    row_part = row_qkv.reshape(seq_count, tok_count, half, 3, HEAD_DIM)
+    row_part = jnp.transpose(row_part, (0, 2, 3, 1, 4))
     places = jnp.arange(tok_count)
     row_mask = (places[:, None] // COLS == places[None, :] // COLS) & (
         places[:, None] >= places[None, :]

time: 208 us -> 198 us (0.952)
  waiting for transfers between devices: 88.4 us -> 75.5 us
  local copies, waits for them, and re-layouts: 54.7 us -> 58.8 us
    all_to_all x1, waiting for transfers between devices: 22.2 us -> 9.56 us  [on_device(): lax.all_to_all(col_packed, SEQ, split_axis=2, concat_axis=1, tiled=True)]
    convert_element_type x0 -> x3, local copies, waits for them, and re-layouts: none -> 6.23 us  [the longest x2 3.87 us: on_device(): col_qkv = jnp.concatenate([project(flat, w_qkv.shape[0], tuple((a[:, spli...]
    reshape x2 -> x1, local copies, waits for them, and re-layouts: 5.55 us -> 2.37 us  [on_device(): row_part = row_qkv.reshape(seq_count, tok_count, half, 3, HEAD_DIM)]
    concatenate x1 -> x0, local copies, waits for them, and re-layouts: 3 us -> none  [on_device(): qkv = jnp.concatenate(pieces, axis=1).astype(jnp.bfloat16)]
    reshape x2, local copies, waits for them, and re-layouts: 0.91 us -> 3.65 us  [column_heads(): flat = packed.reshape(seq_count, length, count, 3, width // 3)]
    slice x1 -> x2, local copies, waits for them, and re-layouts: 1.34 us -> 3.5 us  [the longest x1 2.21 us: on_device(): a[:, :split]]
    dot_general x3 -> x4, matrix products: 8.74 us -> 6.75 us  [project(): return first + jnp.dot(other, other_w, preferred_element_type=jnp.float32)]
    dot_general x3 -> x4, matrix products: 7.62 us -> 8.94 us  [project(): first = jnp.dot(own, own_w, preferred_element_type=jnp.float32)]
  transfers between devices with their start and end apart: 17 -> 17, of which waited for: 9 -> 9; matrix products, arithmetic and copies ran while one was open for 19% -> 27% of each run, Pallas kernels for 0% -> 0%
where the time goes in v3:
time: 198 us; the launch traced here: 197 us
  waiting for transfers between devices  75.5 us (38%)
  local copies, waits for them, and re-layouts  58.8 us (30%)
  starting transfers between devices  34.9 us (18%)
  matrix products  24 us (12%)
  other arithmetic  3.46 us (2%)
    ppermute x8, waiting for transfers between devices, ring(): fwd = lax.ppermute(fwd, axis, [(i, (i + 1) % n) for i in range(n)])  40.2 us
    all_to_all x1, waiting for transfers between devices, on_device(): along_z = lax.all_to_all(spread, 'z', 0, 0, tiled=True)  18 us
    all_to_all x1, waiting for transfers between devices, on_device(): lax.all_to_all(col_packed, SEQ, split_axis=2, concat_axis=1, tiled=True)  9.56 us
    all_to_all x1, starting transfers between devices, on_device(): along_z = lax.all_to_all(spread, 'z', 0, 0, tiled=True)  9 us
    dot_general x4, matrix products, project(): first = jnp.dot(own, own_w, preferred_element_type=jnp.float32)  8.94 us
    all_to_all x1, waiting for transfers between devices, column_heads(): return lax.all_to_all(result, SEQ, split_axis=1, concat_axis=2, tiled=True)  7.78 us
    slice x2, local copies, waits for them, and re-layouts, on_device(): own, other = (own[..., :width], other[..., :width])  7.14 us
    ppermute x4, starting transfers between devices, ring(): bwd = lax.ppermute(bwd, axis, [(i, (i - 1) % n) for i in range(n)])  7.1 us
  transfers between devices with their start and end apart: 17, of which 9 were waited for; matrix products, arithmetic and copies ran while one was open for 27% of the time, Pallas kernels for 0%

profile of v3, /device:TPU:1, one launch (start us, length us, event | category | flops | bytes accessed | tf_op | source)
XLA Modules:
  0.0 197.1 jit_solution(16719061775934531550)
XLA Ops:
  2.4 9.0 %all-to-all-start = ((bf16[8,8,4096]{2,1,0:T(8,128)(2,1)}), bf16[8,8,4096]{2,1,0:T(8,128)(2,1)S(1)}, u32[]{:S(2)}, u32[]{:S(2)}) async-start(bf16[8,8,4096]{2,1,0:T(8,128)(2,1)} %broadcast_in_dim.80), calls=%async_computation | async-start | bytes 1048576 | tf_op jit(solution)/shard_map/all_to_all | solution.py:110
  11.4 18.0 %all-to-all-done = bf16[8,8,4096]{2,1,0:T(8,128)(2,1)S(1)} async-done(((bf16[8,8,4096]{2,1,0:T(8,128)(2,1)}), bf16[8,8,4096]{2,1,0:T(8,128)(2,1)S(1)}, u32[]{:S(2)}, u32[]{:S(2)}) %all-to-all-start) | async-done | bytes 524320 | tf_op jit(solution)/shard_map/all_to_all | solution.py:110
  29.4 1.3 collective-permute-start
  30.6 1.5 collective-permute-start.1
  32.1 1.3 collective-permute-start.7
  33.4 1.4 collective-permute-start.8
  35.2 2.9 %collective-permute-done = bf16[8,8,2048]{2,1,0:T(8,128)(2,1)S(1)} collective-permute-done((bf16[8,8,2048]{2,1,0:T(8,128)(2,1)S(1)}, bf16[8,8,2048]{2,1,0:T(8,128)(2,1)S(1)}, u32[]{:S(2)}, u32[]{:S(2)}) %collective-permute-start) | collective-permute-done | bytes 262176 | tf_op jit(solution)/shard_map/ppermute | solution.py:24
  38.0 2.2 %collective-permute-done.7 = bf16[8,8,2048]{2,1,0:T(8,128)(2,1)S(1)} collective-permute-done((bf16[8,8,2048]{2,1,0:T(8,128)(2,1)S(1)}, bf16[8,8,2048]{2,1,0:T(8,128)(2,1)S(1)}, u32[]{:S(2)}, u32[]{:S(2)}) %collective-permute-start.7) | collective-permute-done | bytes 262176 | tf_op jit(solution)/shard_map/ppermute | solution.py:24
  40.4 5.3 %collective-permute-done.2 = bf16[8,8,2048]{2,1,0:T(8,128)(2,1)S(1)} collective-permute-done((bf16[8,8,2048]{2,1,0:T(8,128)(2,1)S(1)}, bf16[8,8,2048]{2,1,0:T(8,128)(2,1)S(1)}, u32[]{:S(2)}, u32[]{:S(2)}) %collective-permute-start.2) | collective-permute-done | bytes 262176 | tf_op jit(solution)/shard_map/ppermute | solution.py:24
  45.8 1.4 collective-permute-start.3
  47.1 1.5 collective-permute-start.4
  48.8 2.7 %collective-permute-start.11 = (bf16[4,8,8,2048]{3,2,1,0:T(8,128)(2,1)S(1)}, bf16[4,8,8,2048]{3,2,1,0:T(8,128)(2,1)S(1)}, u32[]{:S(2)}, u32[]{:S(2)}) collective-permute-start(bf16[4,8,8,2048]{3,2,1,0:T(8,128)(2,1)S(1)} %bitcast_dynamic-update-slice_fusion.8), channel_id=1, source_target_pairs={{0,144},{16,0},{128,16},{144,128},{1,145},{17,1},{129,17},{145,129... | collective-permute-start | bytes 3145736 | tf_op jit(solution)/shard_map/ppermute | solution.py:27
  51.5 2.5 %broadcast.134.clone = bf16[4,4,8,8,2048]{4,3,2,1,0:T(8,128)(2,1)} broadcast(bf16[]{:T(256)} %constant.157.clone.1), dimensions={} | broadcast | bytes 4194306 | tf_op jit(solution)/shard_map/broadcast.8
  55.1 2.5 %broadcast.134.clone.1 = bf16[4,4,8,8,2048]{4,3,2,1,0:T(8,128)(2,1)} broadcast(bf16[]{:T(256)} %constant.157.clone.1), dimensions={} | broadcast | bytes 4194306 | tf_op jit(solution)/shard_map/broadcast.8
  58.7 11.0 %collective-permute-done.3 = bf16[4,8,8,2048]{3,2,1,0:T(8,128)(2,1)S(1)} collective-permute-done((bf16[4,8,8,2048]{3,2,1,0:T(8,128)(2,1)S(1)}, bf16[4,8,8,2048]{3,2,1,0:T(8,128)(2,1)S(1)}, u32[]{:S(2)}, u32[]{:S(2)}) %collective-permute-start.3) | collective-permute-done | bytes 1048608 | tf_op jit(solution)/shard_map/ppermute | solution.py:24
  70.8 1.3 collective-permute-done.10
  75.2 17.4 %collective-permute-done.5 = bf16[4,8,8,2048]{3,2,1,0:T(8,128)(2,1)S(1)} collective-permute-done((bf16[4,8,8,2048]{3,2,1,0:T(8,128)(2,1)S(1)}, bf16[4,8,8,2048]{3,2,1,0:T(8,128)(2,1)S(1)}, u32[]{:S(2)}, u32[]{:S(2)}) %collective-permute-start.5) | collective-permute-done | bytes 1048608 | tf_op jit(solution)/shard_map/ppermute | solution.py:24
  93.7 3.9 %collective-permute-start.6 = (bf16[4,4,8,8,2048]{4,3,2,1,0:T(8,128)(2,1)}, bf16[4,4,8,8,2048]{4,3,2,1,0:T(8,128)(2,1)}, u32[]{:S(2)}, u32[]{:S(2)}) collective-permute-start(bf16[4,4,8,8,2048]{4,3,2,1,0:T(8,128)(2,1)} %bitcast_dynamic-update-slice_fusion.4), channel_id=1, source_target_pairs={{0,1},{1,0},{2,3},{3,2},{4,5},{5,4},{6,7},{7,6},{8,9},{9,8},{10,11... | collective-permute-start | bytes 12582920 | tf_op jit(solution)/shard_map/ppermute | solution.py:44
  98.6 1.3 collective-permute-start.13
  100.8 1.4 copy.52
  103.7 1.8 fusion.15
  105.5 2.9 %fusion.65 = (bf16[4,4,8,8,1024]{4,3,2,1,0:T(8,128)(2,1)S(1)}, bf16[4,4,8,8,1024]{4,3,2,1,0:T(8,128)(2,1)S(1)}) fusion(bf16[4,4,8,8,2048]{4,3,2,1,0:T(8,128)(2,1)} %bitcast_dynamic-update-slice_fusion.4), kind=kLoop, calls=%fused_computation.108 | loop fusion | bytes 8388608 | tf_op jit(solution)/shard_map/slice | solution.py:120
  109.4 4.3 %fusion.66 = (bf16[4,4,8,8,1024]{4,3,2,1,0:T(8,128)(2,1)S(1)}, bf16[4,4,8,8,1024]{4,3,2,1,0:T(8,128)(2,1)}) fusion(bf16[4,4,8,8,2048]{4,3,2,1,0:T(8,128)(2,1)} %collective-permute-done.6), kind=kLoop, calls=%fused_computation.109 | loop fusion | bytes 8388608 | tf_op jit(solution)/shard_map/slice | solution.py:120
  113.7 1.3 slice.67
  116.9 1.2 convert_element_type.37
  118.1 2.7 %copy.55 = bf16[1,4,96,4,384]{4,3,1,0,2:T(4,128)(2,1)} copy(bf16[1,4,96,4,384]{4,3,2,1,0:T(4,128)(2,1)} %convert_element_type.37) | data formatting | bytes 2359296 | tf_op jit(solution)/shard_map/convert_element_type | solution.py:130
  120.8 3.9 %all-to-all-start.1 = ((bf16[1,4,96,4,384]{4,3,1,0,2:T(4,128)(2,1)}), bf16[1,4,96,4,384]{4,3,1,0,2:T(4,128)(2,1)S(1)}, u32[]{:S(2)}, u32[]{:S(2)}) async-start(bf16[1,4,96,4,384]{4,3,1,0,2:T(4,128)(2,1)} %copy.55), calls=%async_computation.1 | async-start | bytes 2359296 | tf_op jit(solution)/shard_map/all_to_all | solution.py:141
  125.6 3.5 %fusion.2 = f32[384,1536]{1,0:T(8,128)S(1)} fusion(bf16[1024,2048]{1,0:T(8,128)(2,1)} %bitcast.21, bf16[384,2,1024]{0,2,1:T(8,128)(2,1)} %bitcast.194, s32[]{:T(128)S(6)} %select_n.148), kind=kOutput, calls=%fused_computation.2 | convolution fusion | flops 1207959552 | bytes 6291460 | tf_op jit(solution)/shard_map/dot_general | solution.py:69
  129.2 2.2 %slice.71 = bf16[1024,1536]{1,0:T(8,128)(2,1)S(1)} slice(bf16[1024,2048]{1,0:T(8,128)(2,1)} %bitcast.16), slice={[0:1024], [0:1536]} | slice | bytes 6291456 | tf_op jit(solution)/shard_map/slice | solution.py:132
  131.5 1.4 fusion.21
  133.0 1.4 add_convert_fusion.1
  134.4 2.4 %copy.58 = bf16[384,1536]{0,1:T(8,128)(2,1)} copy(bf16[384,1536]{1,0:T(8,128)(2,1)} %add_convert_fusion.1) | data formatting | bytes 2359296 | tf_op jit(solution)/shard_map/convert_element_type | solution.py:133
  136.7 2.4 %copy.59 = bf16[1,384,4,3,128]{4,1,2,3,0:T(8,128)(2,1)} copy(bf16[1,384,4,3,128]{1,4,3,2,0:T(8,128)(2,1)} %bitcast.189) | data formatting | bytes 2359296 | tf_op jit(solution)/shard_map/reshape | solution.py:142
  139.1 2.1 %fusion.68 = f32[4,384]{1,0:T(4,128)S(1)} fusion(pred[384,384]{0,1:T(8,128)(4,1)} %fusion.34, bf16[1,4,3,384,128]{4,3,1,2,0:T(8,128)(2,1)} %bitcast.199), kind=kOutput, calls=%fused_computation.111 | convolution fusion | flops 153354624 | bytes 940032 | tf_op jit(solution)/shard_map/sub | solution.py:80
  141.2 3.3 %fusion.7 = bf16[1,4,384,128]{3,2,1,0:T(8,128)(2,1)} fusion(f32[4,384]{1,0:T(4,128)S(1)} %fusion.68, bf16[1,4,3,384,128]{4,3,1,2,0:T(8,128)(2,1)} %bitcast.200, pred[384,384]{0,1:T(8,128)(4,1)} %fusion.34), kind=kOutput, calls=%fused_computation.18 | convolution fusion | flops 305137536 | bytes 1726464 | tf_op jit(solution)/shard_map/shqk,shkd->shqd/dot_general | solution.py:82
  144.5 9.6 %all-to-all-done.1 = bf16[1,4,96,4,384]{4,3,1,0,2:T(4,128)(2,1)S(1)} async-done(((bf16[1,4,96,4,384]{4,3,1,0,2:T(4,128)(2,1)}), bf16[1,4,96,4,384]{4,3,1,0,2:T(4,128)(2,1)S(1)}, u32[]{:S(2)}, u32[]{:S(2)}) %all-to-all-start.1) | async-done | bytes 1179680 | tf_op jit(solution)/shard_map/all_to_all | solution.py:141
  154.9 1.9 reshape.207
  156.8 1.8 copy.75
  159.5 2.1 %fusion.8 = bf16[1,384,4,128]{3,1,2,0:T(8,128)(2,1)} fusion(f32[4,384]{1,0:T(4,128)S(1)} %fusion.69, bf16[1,4,3,384,128]{4,3,1,2,0:T(8,128)(2,1)S(1)} %bitcast.202, pred[384,384]{0,1:T(8,128)(4,1)S(1)} %fusion.33), kind=kOutput, calls=%fused_computation.19 | convolution fusion | flops 305137536 | bytes 1726464 | tf_op jit(solution)/shard_map/shqk,shkd->shqd/dot_general | solution.py:82
  161.5 2.1 %copy.63 = bf16[1,384,4,128]{3,2,1,0:T(4,128)(2,1)} copy(bf16[1,384,4,128]{3,1,2,0:T(8,128)(2,1)} %fusion.8) | data formatting | bytes 786432 | tf_op jit(solution)/shard_map/transpose | solution.py:97
  163.6 5.6 %all-to-all-start.2 = ((bf16[1,128,3,4,128]{4,3,2,0,1:T(4,128)(2,1)}), bf16[1,128,3,4,128]{4,3,2,0,1:T(4,128)(2,1)S(1)}, u32[]{:S(2)}, u32[]{:S(2)}) async-start(bf16[1,128,3,4,128]{4,3,2,0,1:T(4,128)(2,1)} %bitcast.46), calls=%async_computation.2 | async-start | bytes 786432 | tf_op jit(solution)/shard_map/all_to_all | solution.py:100
  169.2 2.2 %reshape_reshape.17 = bf16[512,2048]{1,0:T(8,128)(2,1)} reshape(bf16[4,4,8,8,1024]{4,3,2,1,0:T(8,128)(2,1)S(1)} %get-tuple-element.26) | data formatting | bytes 4194304 | tf_op jit(solution)/shard_map/reshape;reshape | solution.py:137
  171.4 4.1 %reshape_reshape.14 = bf16[512,2048]{1,0:T(8,128)(2,1)} reshape(bf16[4,4,8,8,1024]{4,3,2,1,0:T(8,128)(2,1)} %get-tuple-element.28) | data formatting | bytes 4194304 | tf_op jit(solution)/shard_map/reshape;reshape | solution.py:137
  175.5 7.8 %all-to-all-done.2 = bf16[1,128,3,4,128]{4,3,2,0,1:T(4,128)(2,1)S(1)} async-done(((bf16[1,128,3,4,128]{4,3,2,0,1:T(4,128)(2,1)}), bf16[1,128,3,4,128]{4,3,2,0,1:T(4,128)(2,1)S(1)}, u32[]{:S(2)}, u32[]{:S(2)}) %all-to-all-start.2) | async-done | bytes 393248 | tf_op jit(solution)/shard_map/all_to_all | solution.py:100
  185.2 2.5 %constant_dynamic-slice_fusion = (bf16[384,1,512]{0,1,2:T(2,128)(2,1)}, bf16[384,1,512]{0,1,2:T(2,128)(2,1)S(1)}) fusion(bf16[384,2,512]{0,1,2:T(2,128)(2,1)S(1)} %bitcast.186, s32[]{:T(128)S(6)} %select_n.149, s32[]{:T(128)S(6)} %select_n.148), kind=kLoop, calls=%fused_computation.82 | loop fusion | bytes 1572872 | tf_op jit(solution)/shard_map/jit(dynamic_index_in_dim)/dynamic_slice | solution.py:62
  188.7 2.6 %fusion.39 = f32[384,2048]{1,0:T(8,128)S(1)} fusion(bf16[512,2048]{1,0:T(8,128)(2,1)} %reshape_reshape.17, bf16[384,1,512]{2,0,1:T(8,128)(2,1)S(1)} %copy.70), kind=kOutput, calls=%fused_computation.69 | convolution fusion | flops 805306368 | bytes 5636096 | tf_op jit(solution)/shard_map/dot_general | solution.py:69
  191.2 2.2 %copy.71 = bf16[384,1,512]{2,0,1:T(8,128)(2,1)S(1)} copy(bf16[384,1,512]{0,1,2:T(2,128)(2,1)} %get-tuple-element.29) | data formatting | bytes 786432 | tf_op jit(solution)/shard_map/jit(dynamic_index_in_dim)/dynamic_slice | solution.py:62
  193.4 3.7 %fusion.6 = bf16[1,384,2048]{2,1,0:T(8,128)(2,1)} fusion(f32[384,2048]{1,0:T(8,128)S(1)} %fusion.39, bf16[512,2048]{1,0:T(8,128)(2,1)} %reshape_reshape.14, bf16[384,1,512]{2,0,1:T(8,128)(2,1)S(1)} %copy.71), kind=kOutput, calls=%fused_computation.14 | convolution fusion | flops 806879232 | bytes 7208960 | tf_op jit(solution)/shard_map/dot_general | solution.py:71
  (68 shorter events, 22.2 us)
Async XLA Ops:
  2.4 27.0 %all-to-all-start = ((bf16[8,8,4096]{2,1,0:T(8,128)(2,1)}), bf16[8,8,4096]{2,1,0:T(8,128)(2,1)S(1)}, u32[]{:S(2)}, u32[]{:S(2)}) async-start(bf16[8,8,4096]{2,1,0:T(8,128)(2,1)} %broadcast_in_dim.80), calls=%async_computation | async-start | bytes 1048576 | tf_op jit(solution)/shard_map/all_to_all | solution.py:110
  29.4 8.7 %collective-permute-start = (bf16[8,8,2048]{2,1,0:T(8,128)(2,1)S(1)}, bf16[8,8,2048]{2,1,0:T(8,128)(2,1)S(1)}, u32[]{:S(2)}, u32[]{:S(2)}) collective-permute-start(bf16[8,8,2048]{2,1,0:T(8,128)(2,1)S(1)} %get-tuple-element.32), channel_id=1, source_target_pairs={{0,16},{16,128},{128,144},{144,0},{1,17},{17,129},{129,145},{145,1... | collective-permute-start | bytes 786440 | tf_op jit(solution)/shard_map/ppermute | solution.py:24
  30.6 9.7 %collective-permute-start.1 = (bf16[8,8,2048]{2,1,0:T(8,128)(2,1)S(1)}, bf16[8,8,2048]{2,1,0:T(8,128)(2,1)S(1)}, u32[]{:S(2)}, u32[]{:S(2)}) collective-permute-start(bf16[8,8,2048]{2,1,0:T(8,128)(2,1)S(1)} %get-tuple-element.32), channel_id=1, source_target_pairs={{0,144},{16,0},{128,16},{144,128},{1,145},{17,1},{129,17},{145,129... | collective-permute-start | bytes 786440 | tf_op jit(solution)/shard_map/ppermute | solution.py:27
  32.1 8.1 %collective-permute-start.7 = (bf16[8,8,2048]{2,1,0:T(8,128)(2,1)S(1)}, bf16[8,8,2048]{2,1,0:T(8,128)(2,1)S(1)}, u32[]{:S(2)}, u32[]{:S(2)}) collective-permute-start(bf16[8,8,2048]{2,1,0:T(8,128)(2,1)S(1)} %get-tuple-element.31), channel_id=1, source_target_pairs={{0,32},{32,64},{64,96},{96,0},{1,33},{33,65},{65,97},{97,1},{2,34}... | collective-permute-start | bytes 786440 | tf_op jit(solution)/shard_map/ppermute | solution.py:24
  33.4 7.0 %collective-permute-start.8 = (bf16[8,8,2048]{2,1,0:T(8,128)(2,1)S(1)}, bf16[8,8,2048]{2,1,0:T(8,128)(2,1)S(1)}, u32[]{:S(2)}, u32[]{:S(2)}) collective-permute-start(bf16[8,8,2048]{2,1,0:T(8,128)(2,1)S(1)} %get-tuple-element.31), channel_id=1, source_target_pairs={{0,96},{32,0},{64,32},{96,64},{1,97},{33,1},{65,33},{97,65},{2,98}... | collective-permute-start | bytes 786440 | tf_op jit(solution)/shard_map/ppermute | solution.py:27
  38.0 7.7 %collective-permute-start.2 = (bf16[8,8,2048]{2,1,0:T(8,128)(2,1)S(1)}, bf16[8,8,2048]{2,1,0:T(8,128)(2,1)S(1)}, u32[]{:S(2)}, u32[]{:S(2)}) collective-permute-start(bf16[8,8,2048]{2,1,0:T(8,128)(2,1)S(1)} %collective-permute-done), channel_id=1, source_target_pairs={{0,16},{16,128},{128,144},{144,0},{1,17},{17,129},{129,145},{145,1... | collective-permute-start | bytes 786440 | tf_op jit(solution)/shard_map/ppermute | solution.py:24
  40.3 8.4 %collective-permute-start.9 = (bf16[8,8,2048]{2,1,0:T(8,128)(2,1)S(1)}, bf16[8,8,2048]{2,1,0:T(8,128)(2,1)S(1)}, u32[]{:S(2)}, u32[]{:S(2)}) collective-permute-start(bf16[8,8,2048]{2,1,0:T(8,128)(2,1)S(1)} %collective-permute-done.7), channel_id=1, source_target_pairs={{0,32},{32,64},{64,96},{96,0},{1,33},{33,65},{65,97},{97,1},{2,34}... | collective-permute-start | bytes 786440 | tf_op jit(solution)/shard_map/ppermute | solution.py:24
  45.8 23.9 %collective-permute-start.3 = (bf16[4,8,8,2048]{3,2,1,0:T(8,128)(2,1)S(1)}, bf16[4,8,8,2048]{3,2,1,0:T(8,128)(2,1)S(1)}, u32[]{:S(2)}, u32[]{:S(2)}) collective-permute-start(bf16[4,8,8,2048]{3,2,1,0:T(8,128)(2,1)S(1)} %bitcast_dynamic-update-slice_fusion.12), channel_id=1, source_target_pairs={{0,32},{32,64},{64,96},{96,0},{1,33},{33,65},{65,97},{97,1},{2,34}... | collective-permute-start | bytes 3145736 | tf_op jit(solution)/shard_map/ppermute | solution.py:24
  47.1 26.0 %collective-permute-start.4 = (bf16[4,8,8,2048]{3,2,1,0:T(8,128)(2,1)S(1)}, bf16[4,8,8,2048]{3,2,1,0:T(8,128)(2,1)S(1)}, u32[]{:S(2)}, u32[]{:S(2)}) collective-permute-start(bf16[4,8,8,2048]{3,2,1,0:T(8,128)(2,1)S(1)} %bitcast_dynamic-update-slice_fusion.12), channel_id=1, source_target_pairs={{0,96},{32,0},{64,32},{96,64},{1,97},{33,1},{65,33},{97,65},{2,98}... | collective-permute-start | bytes 3145736 | tf_op jit(solution)/shard_map/ppermute | solution.py:27
  48.7 23.4 %collective-permute-start.10 = (bf16[4,8,8,2048]{3,2,1,0:T(8,128)(2,1)S(1)}, bf16[4,8,8,2048]{3,2,1,0:T(8,128)(2,1)S(1)}, u32[]{:S(2)}, u32[]{:S(2)}) collective-permute-start(bf16[4,8,8,2048]{3,2,1,0:T(8,128)(2,1)S(1)} %bitcast_dynamic-update-slice_fusion.8), channel_id=1, source_target_pairs={{0,16},{16,128},{128,144},{144,0},{1,17},{17,129},{129,145},{145,1... | collective-permute-start | bytes 3145736 | tf_op jit(solution)/shard_map/ppermute | solution.py:24
  48.8 25.4 %collective-permute-start.11 = (bf16[4,8,8,2048]{3,2,1,0:T(8,128)(2,1)S(1)}, bf16[4,8,8,2048]{3,2,1,0:T(8,128)(2,1)S(1)}, u32[]{:S(2)}, u32[]{:S(2)}) collective-permute-start(bf16[4,8,8,2048]{3,2,1,0:T(8,128)(2,1)S(1)} %bitcast_dynamic-update-slice_fusion.8), channel_id=1, source_target_pairs={{0,144},{16,0},{128,16},{144,128},{1,145},{17,1},{129,17},{145,129... | collective-permute-start | bytes 3145736 | tf_op jit(solution)/shard_map/ppermute | solution.py:27
  69.7 22.9 %collective-permute-start.5 = (bf16[4,8,8,2048]{3,2,1,0:T(8,128)(2,1)S(1)}, bf16[4,8,8,2048]{3,2,1,0:T(8,128)(2,1)S(1)}, u32[]{:S(2)}, u32[]{:S(2)}) collective-permute-start(bf16[4,8,8,2048]{3,2,1,0:T(8,128)(2,1)S(1)} %collective-permute-done.3), channel_id=1, source_target_pairs={{0,32},{32,64},{64,96},{96,0},{1,33},{33,65},{65,97},{97,1},{2,34}... | collective-permute-start | bytes 3145736 | tf_op jit(solution)/shard_map/ppermute | solution.py:24
  72.1 25.5 %collective-permute-start.12 = (bf16[4,8,8,2048]{3,2,1,0:T(8,128)(2,1)S(1)}, bf16[4,8,8,2048]{3,2,1,0:T(8,128)(2,1)S(1)}, u32[]{:S(2)}, u32[]{:S(2)}) collective-permute-start(bf16[4,8,8,2048]{3,2,1,0:T(8,128)(2,1)S(1)} %collective-permute-done.10), channel_id=1, source_target_pairs={{0,16},{16,128},{128,144},{144,0},{1,17},{17,129},{129,145},{145,1... | collective-permute-start | bytes 3145736 | tf_op jit(solution)/shard_map/ppermute | solution.py:24
  75.2 24.7 %copy-start.1 = (bf16[1,384,2048]{2,1,0:T(8,128)(2,1)S(1)}, bf16[1,384,2048]{2,1,0:T(8,128)(2,1)}, u32[]{:S(2)}) copy-start(bf16[1,384,2048]{2,1,0:T(8,128)(2,1)} %param.3) | copy-start | bytes 4718596
  93.7 15.7 %collective-permute-start.6 = (bf16[4,4,8,8,2048]{4,3,2,1,0:T(8,128)(2,1)}, bf16[4,4,8,8,2048]{4,3,2,1,0:T(8,128)(2,1)}, u32[]{:S(2)}, u32[]{:S(2)}) collective-permute-start(bf16[4,4,8,8,2048]{4,3,2,1,0:T(8,128)(2,1)} %bitcast_dynamic-update-slice_fusion.4), channel_id=1, source_target_pairs={{0,1},{1,0},{2,3},{3,2},{4,5},{5,4},{6,7},{7,6},{8,9},{9,8},{10,11... | collective-permute-start | bytes 12582920 | tf_op jit(solution)/shard_map/ppermute | solution.py:44
  98.6 15.1 %collective-permute-start.13 = (bf16[4,4,8,8,2048]{4,3,2,1,0:T(8,128)(2,1)}, bf16[4,4,8,8,2048]{4,3,2,1,0:T(8,128)(2,1)}, u32[]{:S(2)}, u32[]{:S(2)}) collective-permute-start(bf16[4,4,8,8,2048]{4,3,2,1,0:T(8,128)(2,1)} %bitcast_dynamic-update-slice_fusion), channel_id=1, source_target_pairs={{0,1},{1,0},{2,3},{3,2},{4,5},{5,4},{6,7},{7,6},{8,9},{9,8},{10,11... | collective-permute-start | bytes 12582920 | tf_op jit(solution)/shard_map/ppermute | solution.py:44
  102.5 1.2 copy-start.2
  105.5 2.9 %copy-start = (bf16[384,2,4,2,2,8,8]{0,6,5,4,3,2,1:T(8,128)(2,1)S(1)}, bf16[384,2,4,2,2,8,8]{0,6,5,4,3,2,1:T(8,128)(2,1)}, u32[]{:S(2)}) copy-start(bf16[384,2,4,2,2,8,8]{0,6,5,4,3,2,1:T(8,128)(2,1)} %copy.52) | copy-start | bytes 4718596
  109.4 5.6 %copy-start.3 = (bf16[384,2,2,2,4,8,8]{0,6,5,4,3,2,1:T(8,128)(2,1)S(1)}, bf16[384,2,2,2,4,8,8]{0,6,5,4,3,2,1:T(8,128)(2,1)}, u32[]{:S(2)}) copy-start(bf16[384,2,2,2,4,8,8]{0,6,5,4,3,2,1:T(8,128)(2,1)} %copy-done.2) | copy-start | bytes 4718596
  120.8 33.3 %all-to-all-start.1 = ((bf16[1,4,96,4,384]{4,3,1,0,2:T(4,128)(2,1)}), bf16[1,4,96,4,384]{4,3,1,0,2:T(4,128)(2,1)S(1)}, u32[]{:S(2)}, u32[]{:S(2)}) async-start(bf16[1,4,96,4,384]{4,3,1,0,2:T(4,128)(2,1)} %copy.55), calls=%async_computation.1 | async-start | bytes 2359296 | tf_op jit(solution)/shard_map/all_to_all | solution.py:141
  129.2 2.4 %copy-start.4 = (bf16[384,2,2,2,4,8,8]{0,6,5,4,3,2,1:T(8,128)(2,1)S(1)}, bf16[384,2,2,2,4,8,8]{0,6,5,4,3,2,1:T(8,128)(2,1)}, u32[]{:S(2)}) copy-start(bf16[384,2,2,2,4,8,8]{0,6,5,4,3,2,1:T(8,128)(2,1)} %copy-done.2) | copy-start | bytes 4718596
  163.6 19.7 %all-to-all-start.2 = ((bf16[1,128,3,4,128]{4,3,2,0,1:T(4,128)(2,1)}), bf16[1,128,3,4,128]{4,3,2,0,1:T(4,128)(2,1)S(1)}, u32[]{:S(2)}, u32[]{:S(2)}) async-start(bf16[1,128,3,4,128]{4,3,2,0,1:T(4,128)(2,1)} %bitcast.46), calls=%async_computation.2 | async-start | bytes 786432 | tf_op jit(solution)/shard_map/all_to_all | solution.py:100
  171.4 12.3 %copy-start.5 = (bf16[1,4,384,128]{3,2,1,0:T(8,128)(2,1)S(1)}, bf16[1,4,384,128]{3,2,1,0:T(8,128)(2,1)}, u32[]{:S(2)}) copy-start(bf16[1,4,384,128]{3,2,1,0:T(8,128)(2,1)} %fusion.7) | copy-start | bytes 1179652
